TPU v7x, 512 devices: a whole 4x8x8 slice. The times are simulated.
512 devices in a mesh: gx: 8 (over z_lo, x), gy: 16 (over y, core), gz: 4 (over z_hi).
Axes of the slice: x: 4, y: 8, z: 8 (z_hi: 4, z_lo: 2; z = z_hi * 2 + z_lo), core: 2. Of those that a mesh axis runs over, the one named last changes fastest.
Arguments:
- positions: float32 [3, 262144], P(None, ('gx', 'gy', 'gz')), may hold values from 0 to 1
- velocities: float32 [3, 262144], P(None, ('gx', 'gy', 'gz')), may hold values from -5 to 5
- neighbour_index: int32 [24, 262144], P(None, ('gx', 'gy', 'gz')), may hold values from 0 to 3967, as said below
- neighbour_count: int32 [262144], P(('gx', 'gy', 'gz')), may hold values from 0 to 24, as said below
- ghost_list: int32 [65536], P(('gx', 'gy', 'gz')), may hold values from 0 to 511, as said below
- brick_count: int32 [512], P(('gx', 'gy', 'gz')), may hold values from 128 to 512, as said below
- atom_cell: int32 [262144], P(('gx', 'gy', 'gz')), may hold values from 0 to 127
- radial_weight: float32 [16, 8], replicated, may hold values from -2 to 2
- linear_weight: float32 [16], replicated, may hold values from -4 to 4
- pair_coupling: float32 [4, 16, 16], replicated, may hold values from -0.375 to 0.375
- electron_temp: float32 [16, 64, 64], P('gz', 'gy', 'gx'), may hold values from 1 to 2
- conductivity: float32 [16, 64, 64], P('gz', 'gy', 'gx'), may hold values from 0.3 to 1
- heating: float32 [16, 64, 64], P('gz', 'gy', 'gx'), may hold values from 0.05 to 1
Outputs:
- forces: float32 [3, 262144], P(None, ('gx', 'gy', 'gz'))
- new_velocity: float32 [3, 262144], P(None, ('gx', 'gy', 'gz'))
- new_electron_temp: float32 [16, 64, 64], P('gz', 'gy', 'gx')
- totals: float32 [10], replicated
Inputs may be any that keep to these rules, and one draw needn't show every extreme that they name: `brick_count`: bricks with b % 4 == 3 are full. `ghost_list`: entries of brick b name live atoms of brick b. `neighbour_count`: zero for atoms that are not live, at least 12 for live ones. `neighbour_index`: A used entry below 512 names a live atom of the same brick; otherwise it is 512 + s * 128 + g with slot s != 13, and never a slot whose depth offset crosses the film's surface (o2 = -1 in bricks with bz = 0, o2 = 1 in bricks with bz = 3).
All inputs are finite; a program needn't handle non-finite values.
Results may differ from a plain program's by a relative error of at most 0.0003.
Values sent between devices are 32-bit elements; how exact they have to be, the bound alone decides.
No kernel may reach another device: no remote copies, remote signals or barrier semaphores. Data moves between devices by JAX's collectives and lax.ppermute only.
A program may use at most 64 MiB of HBM per device.

v0:
```python
import functools

import jax
import jax.numpy as jnp
from jax import lax
from jax.sharding import Mesh
from jax.sharding import PartitionSpec as P

SUBSTEPS = 4
GX_GY_GZ = ("gx_0", "gx_1", "gy_0", "gy_1", "gz")
GX = ("gx_0", "gx_1")
GY = ("gy_0", "gy_1")


HEAT_STEP = 0.15
COUPLE = 0.5
RELAX = 0.2
KICK = 0.05
SPREAD = 2.0
ROOT_THREE = 1.7320508


def padded(cells, sides, width):
    for axis, dim in sides:
        count = lax.axis_size(axis)
        head = lax.slice_in_dim(cells, 0, width, axis=dim)
        tail = lax.slice_in_dim(cells, cells.shape[dim] - width, cells.shape[dim], axis=dim)
        cells = jnp.concatenate(
            [
                lax.ppermute(tail, axis, [(i, (i + 1) % count) for i in range(count)]),
                cells,
                lax.ppermute(head, axis, [((i + 1) % count, i) for i in range(count)]),
            ],
            axis=dim,
        )
    return cells


def by_axis(shard, axes):
    return functools.reduce(lax.psum, axes, shard)


def harmonics(vector):
    coord_x, coord_y, coord_z = (vector[0], vector[1], vector[2])
    radius_sq = coord_x * coord_x + coord_y * coord_y + coord_z * coord_z
    terms = [
        jnp.ones_like(coord_x),
        coord_x,
        coord_y,
        coord_z,
        ROOT_THREE * coord_x * coord_y,
        ROOT_THREE * coord_y * coord_z,
        0.5 * (3.0 * coord_z * coord_z - radius_sq),
        ROOT_THREE * coord_x * coord_z,
        0.5 * ROOT_THREE * (coord_x * coord_x - coord_y * coord_y),
        0.79 * coord_y * (3.0 * coord_x * coord_x - coord_y * coord_y),
        3.87 * coord_x * coord_y * coord_z,
        0.61 * coord_y * (4.0 * coord_z * coord_z - coord_x * coord_x - coord_y * coord_y),
        0.5
        * coord_z
        * (2.0 * coord_z * coord_z - 3.0 * coord_x * coord_x - 3.0 * coord_y * coord_y),
        0.61 * coord_x * (4.0 * coord_z * coord_z - coord_x * coord_x - coord_y * coord_y),
        1.94 * coord_z * (coord_x * coord_x - coord_y * coord_y),
        0.79 * coord_x * (coord_x * coord_x - 3.0 * coord_y * coord_y),
    ]
    return jnp.stack(terms)


def radial(vector, orders):
    radius_sq = jnp.sum(vector * vector, axis=0)
    decay = jnp.exp(-radius_sq / SPREAD)
    argument = 2.0 * decay - 1.0
    polys = [jnp.ones_like(argument), argument]
    for order_id in range(2, orders):
        polys.append(2.0 * argument * polys[-1] - polys[-2])
    return decay * jnp.stack(polys[:orders])


def pair_energy(vector, weights):
    basis = radial(vector, weights.shape[0])
    mixed = jnp.sum(weights * basis[:, None], axis=0)
    return jnp.sum(mixed * harmonics(vector), axis=0)


def atom_basis(separation, pair_mask, radial_weight):
    basis = radial(separation, radial_weight.shape[1])
    shaped = (
        jnp.einsum("nc,cka->nka", radial_weight, basis, precision=lax.Precision.HIGHEST) * pair_mask
    )
    return jnp.einsum(
        "nka,mka->nma", shaped, harmonics(separation), precision=lax.Precision.HIGHEST
    )


def adjoints(basis_sum, linear_weight, pair_coupling):
    per_harmonic = jnp.concatenate(
        [
            jnp.repeat(pair_coupling[degree_id : degree_id + 1], copies, axis=0)
            for degree_id, copies in enumerate((1, 3, 5, 7))
        ],
        axis=0,
    )
    forward = jnp.einsum("mnp,pma->nma", per_harmonic, basis_sum, precision=lax.Precision.HIGHEST)
    backward = jnp.einsum("mpn,pma->nma", per_harmonic, basis_sum, precision=lax.Precision.HIGHEST)
    energy = jnp.dot(linear_weight, basis_sum[:, 0, :], precision=lax.Precision.HIGHEST) + jnp.sum(
        basis_sum * forward, axis=(0, 1)
    )
    adjoint = (forward + backward).at[:, 0, :].add(linear_weight[:, None])
    return (energy, adjoint)


def pair_forces(separation, pair_mask, own_weights, other_weights):
    own_grad = jax.grad(lambda vector: jnp.sum(pair_energy(vector, own_weights)))(separation)
    other_grad = jax.grad(lambda vector: jnp.sum(pair_energy(vector, other_weights)))(-separation)
    pieces = (own_grad - other_grad) * pair_mask
    return (
        jnp.sum(pieces, axis=1),
        jnp.einsum("aki,bki->ab", separation, pieces, precision=lax.Precision.HIGHEST),
    )


def substep(temp_ext, kappa_ext, heat_here, lattice_here, occupancy_here, lower_open, upper_open):
    centre = temp_ext[1:-1, 1:-1, 1:-1]
    centre_kappa = kappa_ext[1:-1, 1:-1, 1:-1]

    def face(beside_temp, beside_kappa):
        return 0.5 * (centre_kappa + beside_kappa) * (beside_temp - centre)

    divergence = (
        face(temp_ext[1:-1, 1:-1, 2:], kappa_ext[1:-1, 1:-1, 2:])
        + face(temp_ext[1:-1, 1:-1, :-2], kappa_ext[1:-1, 1:-1, :-2])
        + face(temp_ext[1:-1, 2:, 1:-1], kappa_ext[1:-1, 2:, 1:-1])
        + face(temp_ext[1:-1, :-2, 1:-1], kappa_ext[1:-1, :-2, 1:-1])
        + face(temp_ext[2:, 1:-1, 1:-1], kappa_ext[2:, 1:-1, 1:-1]) * upper_open
        + face(temp_ext[:-2, 1:-1, 1:-1], kappa_ext[:-2, 1:-1, 1:-1]) * lower_open
    )
    return centre + HEAT_STEP / centre * (
        divergence + heat_here - COUPLE * occupancy_here * (centre - lattice_here)
    )


def local(
    positions,
    velocities,
    neighbour_index,
    neighbour_count,
    ghost_list,
    brick_count,
    atom_cell,
    radial_weight,
    linear_weight,
    pair_coupling,
    electron_temp,
    conductivity,
    heating,
):
    atom_slots = positions.shape[1]
    ghosts = ghost_list.shape[0]
    neigh_depth = neighbour_index.shape[0]
    orders = radial_weight.shape[1]
    live_count = brick_count[0]
    alive_mask = (jnp.arange(atom_slots) < live_count).astype(jnp.float32)
    slot_ids = jnp.arange(27)
    offsets = jnp.stack(
        [slot_ids // 9 - 1, slot_ids // 3 % 3 - 1, slot_ids % 3 - 1], axis=1
    ).astype(jnp.float32)
    ghost_sent = jnp.take(positions, ghost_list, axis=1).reshape(1, 1, 1, 3, ghosts)
    framed = padded(ghost_sent, ((GX, 0), (GY, 1), ("gz", 2)), 1)
    shifted = framed.reshape(27, 3, ghosts) + offsets[:, :, None]
    pos_table = jnp.concatenate(
        [positions, jnp.transpose(shifted, (1, 0, 2)).reshape(3, 27 * ghosts)], axis=1
    )
    separation = pos_table[:, neighbour_index] - positions[:, None, :]
    pair_mask = (jnp.arange(neigh_depth)[:, None] < neighbour_count[None, :]).astype(jnp.float32)
    basis_sum = atom_basis(separation, pair_mask, radial_weight)
    energy, adjoint = adjoints(basis_sum, linear_weight, pair_coupling)
    reduced = jnp.einsum("nc,nma->cma", radial_weight, adjoint, precision=lax.Precision.HIGHEST)
    own_table = reduced.reshape(orders * 16, atom_slots)
    picked = jnp.take(own_table, ghost_list, axis=1).reshape(1, 1, 1, orders * 16, ghosts)
    framed_adjoint = padded(picked, ((GX, 0), (GY, 1), ("gz", 2)), 1)
    remote = framed_adjoint.reshape(27, orders * 16, ghosts)
    adjoint_table = jnp.concatenate(
        [own_table, jnp.transpose(remote, (1, 0, 2)).reshape(orders * 16, 27 * ghosts)], axis=1
    )
    block_rows = 128
    live_blocks = (live_count + block_rows - 1) // block_rows

    def one_block(block_id, carry):
        forces_acc, virial_acc = carry
        start = block_id * block_rows
        index_block = lax.dynamic_slice_in_dim(neighbour_index, start, block_rows, 1)
        count_block = lax.dynamic_slice_in_dim(neighbour_count, start, block_rows, 0)
        own_block = lax.dynamic_slice_in_dim(positions, start, block_rows, 1)
        weights_block = lax.dynamic_slice_in_dim(own_table, start, block_rows, 1)
        block_sep = pos_table[:, index_block] - own_block[:, None, :]
        block_mask = (jnp.arange(neigh_depth)[:, None] < count_block[None, :]).astype(jnp.float32)
        other_weights = adjoint_table[:, index_block].reshape(orders, 16, neigh_depth, block_rows)
        block_force, block_virial = pair_forces(
            block_sep, block_mask, weights_block.reshape(orders, 16, 1, block_rows), other_weights
        )
        forces_acc = lax.dynamic_update_slice_in_dim(forces_acc, block_force, start, 1)
        return (forces_acc, virial_acc + block_virial)

    forces, virial = lax.fori_loop(
        0,
        live_blocks,
        one_block,
        (jnp.zeros((3, atom_slots), jnp.float32), jnp.zeros((3, 3), jnp.float32)),
    )
    kicked = velocities + KICK * forces
    grid_shape = electron_temp.shape
    cell_total = grid_shape[0] * grid_shape[1] * grid_shape[2]
    kinetic = jax.ops.segment_sum(
        alive_mask * jnp.sum(kicked * kicked, axis=0), atom_cell, num_segments=cell_total
    )
    filled = jax.ops.segment_sum(alive_mask, atom_cell, num_segments=cell_total)
    lattice = (kinetic / (3.0 * jnp.maximum(filled, 1.0))).reshape(grid_shape)
    occupancy = jnp.minimum(filled, 1.0).reshape(grid_shape)
    depth_index = lax.axis_index("gz")
    depth_total = grid_shape[0] * lax.axis_size("gz")
    stacked = jnp.stack([electron_temp, conductivity, heating, lattice, occupancy])
    margins = padded(stacked, ((GX, 3), (GY, 2), ("gz", 1)), SUBSTEPS)
    electron = margins[0]
    cond_ext = margins[1]
    heat_ext = margins[2]
    lattice_ext = margins[3]
    occupancy_ext = margins[4]
    for substep_id in range(SUBSTEPS):
        margin = SUBSTEPS - substep_id - 1
        heat_ext = heat_ext[1:-1, 1:-1, 1:-1]
        lattice_ext = lattice_ext[1:-1, 1:-1, 1:-1]
        occupancy_ext = occupancy_ext[1:-1, 1:-1, 1:-1]
        global_z = depth_index * grid_shape[0] - margin + jnp.arange(heat_ext.shape[0])
        lower_open = (global_z != 0).astype(jnp.float32)[:, None, None]
        upper_open = (global_z != depth_total - 1).astype(jnp.float32)[:, None, None]
        lower_open, upper_open = (lower_open, upper_open)
        electron = substep(
            electron,
            cond_ext * electron,
            heat_ext,
            lattice_ext,
            occupancy_ext,
            lower_open,
            upper_open,
        )
        cond_ext = cond_ext[1:-1, 1:-1, 1:-1]
    exchange_rate = RELAX * (electron - lattice) / (electron + lattice)
    scaling = jnp.take(exchange_rate.reshape(-1), atom_cell)
    new_velocity = kicked * (1.0 + scaling) * alive_mask
    count_total, energy_total, virial_total = (
        by_axis(live_count.astype(jnp.float32), GX_GY_GZ),
        by_axis(jnp.sum(energy * alive_mask), GX_GY_GZ),
        by_axis(virial, GX_GY_GZ),
    )
    totals = (
        jnp.concatenate([jnp.reshape(energy_total, (1,)), virial_total.reshape(9)]) / count_total
    )
    return (forces, new_velocity, electron, totals)


def solution(mesh):
    torus = Mesh(
        mesh.devices.reshape(2, 4, 8, 2, mesh.shape["gz"]), ("gx_0", "gx_1", "gy_0", "gy_1", "gz")
    )
    placed = (
        P(None, GX_GY_GZ),
        P(None, GX_GY_GZ),
        P(None, GX_GY_GZ),
        P(GX_GY_GZ),
        P(GX_GY_GZ),
        P(GX_GY_GZ),
        P(GX_GY_GZ),
        P(),
        P(),
        P(),
        P("gz", GY, GX),
        P("gz", GY, GX),
        P("gz", GY, GX),
    )
    return jax.shard_map(
        local,
        mesh=torus,
        in_specs=placed,
        out_specs=(P(None, GX_GY_GZ), P(None, GX_GY_GZ), P("gz", GY, GX), P()),
        check_vma=False,
    )
```

profile of v0, /device:TPU:1, one launch (start us, length us, event | category | flops | bytes accessed | tf_op | source)
XLA Modules:
  0.0 410.2 jit_solution(2166476695855586244)
XLA Ops:
  4.2 7.0 %collective-permute-start.1 = (f32[1,1,1,3,128]{3,4,2,1,0:T(8,128)S(1)}, f32[1,1,1,3,128]{3,4,2,1,0:T(8,128)S(1)}, u32[]{:S(2)}, u32[]{:S(2)}) collective-permute-start(f32[1,1,1,3,128]{3,4,2,1,0:T(8,128)S(1)} %bitcast_select_fusion.1), channel_id=1, source_target_pairs={{64,0},{128,64},{192,128},{256,192},{320,256},{384,320},{448,384},... | collective-permute-start | bytes 4616 | tf_op jit(solution)/shard_map/ppermute | solution.py:32
  11.3 1.9 collective-permute-start
  16.4 2.0 collective-permute-done
  18.5 3.3 collective-permute-start.2
  22.5 2.6 collective-permute-done.3
  25.1 5.5 %collective-permute-start.4 = (f32[3,3,1,3,128]{4,2,3,1,0:T(1,128)S(1)}, f32[3,3,1,3,128]{4,2,3,1,0:T(1,128)S(1)}, u32[]{:S(2)}, u32[]{:S(2)}) collective-permute-start(f32[3,3,1,3,128]{4,2,3,1,0:T(1,128)S(1)} %pad_maximum_fusion.12), channel_id=1, source_target_pairs={{0,1},{1,2},{2,3},{3,0},{4,5},{5,6},{6,7},{7,4},{8,9},{9,10},{10,1... | collective-permute-start | bytes 41480 | tf_op jit(solution)/shard_map/ppermute | solution.py:30
  30.6 5.9 %collective-permute-start.5 = (f32[3,3,1,3,128]{4,2,3,1,0:T(1,128)S(1)}, f32[3,3,1,3,128]{4,2,3,1,0:T(1,128)S(1)}, u32[]{:S(2)}, u32[]{:S(2)}) collective-permute-start(f32[3,3,1,3,128]{4,2,3,1,0:T(1,128)S(1)} %pad_maximum_fusion.12), channel_id=1, source_target_pairs={{1,0},{2,1},{3,2},{0,3},{5,4},{6,5},{7,6},{4,7},{9,8},{10,9},{11,1... | collective-permute-start | bytes 41480 | tf_op jit(solution)/shard_map/ppermute | solution.py:32
  39.5 41.2 %gather_fusion.3 = f32[12288,3]{1,0:T(8,128)} fusion(f32[3,3968]{0,1:T(8,128)S(1)} %copy.106, s32[12288]{0:T(1024)S(1)} %broadcast_clamp_fusion), kind=kCustom, calls=%fused_computation.3 | custom fusion | bytes 344064 | tf_op jit(solution)/shard_map/gather | solution.py:173
  80.7 4.4 %copy.122 = f32[24,512,3]{1,0,2:T(8,128)S(1)} copy(f32[24,512,3]{2,1,0:T(8,128)} %bitcast.356) | data formatting | bytes 294912 | tf_op jit(solution)/shard_map/gather | solution.py:173
  86.5 3.8 copy.110
  90.6 3.7 copy.109
  94.3 12.2 %fusion.283 = f32[512,16,16]{2,1,0:T(8,128)} fusion(f32[16,24,512]{1,0,2:T(8,128)} %copy.109, f32[16,24,512]{1,0,2:T(8,128)} %copy.110), kind=kOutput, calls=%fused_computation.627 | convolution fusion | flops 37748736 | bytes 2097152 | tf_op jit(solution)/shard_map/nka,mka->nma/dot_general | solution.py:90
  106.5 3.0 copy.111
  110.7 3.6 copy.115
  114.3 3.7 copy.112
  118.0 6.1 %fusion.141 = (f32[512]{0:T(512)S(1)}, f32[16,16,512]{0,1,2:T(8,128)S(1)}) fusion(f32[16,512,16]{2,0,1:T(8,128)} %copy.112, f32[512,16,16]{2,1,0:T(8,128)} %fusion.283, f32[16,512,16]{2,0,1:T(8,128)} %copy.115), kind=kLoop, calls=%fused_computation.319 | loop fusion | flops 392704 | bytes 2099200 | tf_op jit(solution)/shard_map/reduce_sum | solution.py:105
  124.1 2.0 copy-done.2
  126.2 8.3 %scatter-add.19 = f32[16,16,512]{0,1,2:T(8,128)} dynamic-update-slice(f32[16,16,512]{0,1,2:T(8,128)} %copy-done.2, f32[16,1,512]{0,1,2:T(1,128)S(1)} %slice_add_fusion.2, s32[]{:T(128)} %constant.276.clone.1, s32[]{:T(128)} %constant.276.clone.1, s32[]{:T(128)} %constant.276.clone.1) | dynamic-update-slice | bytes 65540 | tf_op jit(solution)/shard_map/scatter-add | solution.py:108
  134.5 7.2 %fusion.145 = f32[8,16,512]{2,0,1:T(8,128)S(1)} fusion(f32[16,16,512]{0,1,2:T(8,128)} %scatter-add.19, f32[16,8]{0,1:T(8,128)S(1)} %copy-done), kind=kOutput, calls=%fused_computation.326 | convolution fusion | flops 12582912 | bytes 786944 | tf_op jit(solution)/shard_map/nc,nma->cma/dot_general | solution.py:177
  142.7 1.9 collective-permute-start.6
  144.6 5.5 %collective-permute-start.7 = (f32[1,1,1,128,128]{3,4,2,1,0:T(8,128)S(1)}, f32[1,1,1,128,128]{3,4,2,1,0:T(8,128)S(1)}, u32[]{:S(2)}, u32[]{:S(2)}) collective-permute-start(f32[1,1,1,128,128]{3,4,2,1,0:T(8,128)S(1)} %bitcast_select_fusion), channel_id=1, source_target_pairs={{64,0},{128,64},{192,128},{256,192},{320,256},{384,320},{448,384},... | collective-permute-start | bytes 196616 | tf_op jit(solution)/shard_map/ppermute | solution.py:32
  151.5 2.3 collective-permute-start.8
  153.8 2.6 collective-permute-done.8
  156.4 2.8 collective-permute-done.9
  159.2 5.7 %collective-permute-start.10 = (f32[3,3,1,128,128]{3,4,2,1,0:T(8,128)S(1)}, f32[3,3,1,128,128]{3,4,2,1,0:T(8,128)S(1)}, u32[]{:S(2)}, u32[]{:S(2)}) collective-permute-start(f32[3,3,1,128,128]{3,4,2,1,0:T(8,128)S(1)} %pad_maximum_fusion.2), channel_id=1, source_target_pairs={{0,1},{1,2},{2,3},{3,0},{4,5},{5,6},{6,7},{7,4},{8,9},{9,10},{10,1... | collective-permute-start | bytes 1769480 | tf_op jit(solution)/shard_map/ppermute | solution.py:30
  166.9 4.1 scatter_custom_fusion.1
  172.8 17.5 %collective-permute-done.10 = f32[3,3,1,128,128]{3,4,2,1,0:T(8,128)S(1)} collective-permute-done((f32[3,3,1,128,128]{3,4,2,1,0:T(8,128)S(1)}, f32[3,3,1,128,128]{3,4,2,1,0:T(8,128)S(1)}, u32[]{:S(2)}, u32[]{:S(2)}) %collective-permute-start.10) | collective-permute-done | bytes 589856 | tf_op jit(solution)/shard_map/ppermute | solution.py:30
  190.3 5.2 %collective-permute-done.11 = f32[3,3,1,128,128]{3,4,2,1,0:T(8,128)S(1)} collective-permute-done((f32[3,3,1,128,128]{3,4,2,1,0:T(8,128)S(1)}, f32[3,3,1,128,128]{3,4,2,1,0:T(8,128)S(1)}, u32[]{:S(2)}, u32[]{:S(2)}) %collective-permute-start.11) | collective-permute-done | bytes 589856 | tf_op jit(solution)/shard_map/ppermute | solution.py:32
  195.9 66.4 %while.16 = (s32[]{:T(128)}, f32[3,512]{1,0:T(4,128)S(1)}, f32[3,3]{1,0:T(4,128)S(1)}, s32[]{:T(128)}, f32[128,512]{1,0:T(8,128)S(1)}, /*index=5*/s32[24,512]{1,...) while((s32[]{:T(128)}, f32[3,512]{1,0:T(4,128)S(1)}, ...), condition=%wide.region_10.11_spmd, body=%wide.region_1.10_spmd.sunk | while | flops 5894799 | bytes 20975916 | solution.py:204
  196.6 12.4 %gather_fusion = f32[3072,3]{1,0:T(8,128)} fusion(f32[3,3968]{0,1:T(8,128)} %get-tuple-element.426, s32[3072]{0:T(1024)S(1)} %fusion.300), kind=kCustom, calls=%fused_computation.clone.1 | custom fusion | bytes 86016 | tf_op jit(solution)/shard_map/while/body/gather | solution.py:195
  211.3 10.8 %gather_fusion.1 = f32[3072,128]{1,0:T(8,128)} fusion(f32[128,3968]{0,1:T(8,128)S(1)} %get-tuple-element.428, s32[3072]{0:T(1024)S(1)} %fusion.300), kind=kCustom, calls=%fused_computation.1.clone.1 | custom fusion | bytes 3158016 | tf_op jit(solution)/shard_map/while/body/gather | solution.py:197
  222.2 3.0 copy.141
  229.7 12.4 %gather_fusion = f32[3072,3]{1,0:T(8,128)} fusion(f32[3,3968]{0,1:T(8,128)} %get-tuple-element.426, s32[3072]{0:T(1024)S(1)} %fusion.300), kind=kCustom, calls=%fused_computation.clone.1 | custom fusion | bytes 86016 | tf_op jit(solution)/shard_map/while/body/gather | solution.py:195
  244.4 10.8 %gather_fusion.1 = f32[3072,128]{1,0:T(8,128)} fusion(f32[128,3968]{0,1:T(8,128)S(1)} %get-tuple-element.428, s32[3072]{0:T(1024)S(1)} %fusion.300), kind=kCustom, calls=%fused_computation.1.clone.1 | custom fusion | bytes 3158016 | tf_op jit(solution)/shard_map/while/body/gather | solution.py:197
  255.3 3.0 copy.141
  262.3 4.1 scatter_custom_fusion
  266.7 32.2 %collective-permute-start.12 = (f32[5,4,4,4]{3,2,1,0:T(4,128)S(1)}, f32[5,4,4,4]{3,2,1,0:T(4,128)S(1)}, u32[]{:S(2)}, u32[]{:S(2)}) collective-permute-start(f32[5,4,4,4]{3,2,1,0:T(4,128)S(1)} %get-tuple-element.262), channel_id=1, source_target_pairs={{0,64},{64,128},{128,192},{192,256},{256,320},{320,384},{384,448},... | collective-permute-start | bytes 3848 | tf_op jit(solution)/shard_map/ppermute | solution.py:30
  301.1 2.5 collective-permute-done.13
  303.7 39.8 %collective-permute-start.14 = (f32[5,4,4,16]{3,2,1,0:T(4,128)S(1)}, f32[5,4,4,16]{3,2,1,0:T(4,128)S(1)}, u32[]{:S(2)}, u32[]{:S(2)}) collective-permute-start(f32[5,4,4,16]{3,2,1,0:T(4,128)S(1)} %pad_maximum_fusion.11), channel_id=1, source_target_pairs={{0,4},{4,8},{8,12},{12,16},{16,20},{20,24},{24,28},{28,32},{32,36}... | collective-permute-start | bytes 15368 | tf_op jit(solution)/shard_map/ppermute | solution.py:30
  344.1 4.4 %all-reduce.10 = (f32[3,3]{1,0:T(4,128)S(1)}, f32[]{:T(128)}, f32[]{:T(128)}) all-reduce(f32[3,3]{1,0:T(4,128)S(1)} %get-tuple-element.175, f32[]{:T(128)} %select_reduce_fusion, f32[]{:T(128)S(6)} %convert_element_type.102), channel_id=1, replica_groups=mesh['gx_0'=2,'gx_1'=4,'gy_0'=8,'gy_1'=2,'gz'=4] {'gx_0'}, use_global_device_ids=true, to_apply=%region_21.22 | all-reduce | flops 11 | bytes 88 | tf_op jit(solution)/shard_map/psum | solution.py:40
  348.5 9.6 %all-reduce.8 = (f32[3,3]{1,0:T(4,128)S(1)}, f32[]{:T(128)}, f32[]{:T(128)}) all-reduce(f32[3,3]{1,0:T(4,128)S(1)} %get-tuple-element.223, f32[]{:T(128)} %get-tuple-element.224, f32[]{:T(128)} %get-tuple-element.225), channel_id=1, replica_groups=mesh['gx_0'=2,'gx_1'=4,'gy_0'=8,'gy_1'=2,'gz'=4] {'gx_1'}, use_global_device_ids=true, to_apply=%region_22.23 | all-reduce | flops 11 | bytes 88 | tf_op jit(solution)/shard_map/psum | solution.py:40
  358.1 12.9 %all-reduce.6 = (f32[3,3]{1,0:T(4,128)S(1)}, f32[]{:T(128)}, f32[]{:T(128)}) all-reduce(f32[3,3]{1,0:T(4,128)S(1)} %get-tuple-element.217, f32[]{:T(128)} %get-tuple-element.218, f32[]{:T(128)} %get-tuple-element.219), channel_id=1, replica_groups=mesh['gx_0'=2,'gx_1'=4,'gy_0'=8,'gy_1'=2,'gz'=4] {'gy_0'}, use_global_device_ids=true, to_apply=%region_23.24 | all-reduce | flops 11 | bytes 88 | tf_op jit(solution)/shard_map/psum | solution.py:40
  371.0 11.1 %all-reduce.9 = (f32[3,3]{1,0:T(4,128)S(1)}, f32[]{:T(128)}, f32[]{:T(128)}) all-reduce(f32[3,3]{1,0:T(4,128)S(1)} %get-tuple-element.211, f32[]{:T(128)} %get-tuple-element.212, f32[]{:T(128)} %get-tuple-element.213), channel_id=1, replica_groups=mesh['gx_0'=2,'gx_1'=4,'gy_0'=8,'gy_1'=2,'gz'=4] {'gy_1'}, use_global_device_ids=true, to_apply=%region_24.25 | all-reduce | flops 11 | bytes 88 | tf_op jit(solution)/shard_map/psum | solution.py:40
  382.2 9.6 %all-reduce.7 = (f32[9]{0:T(128)S(1)}, f32[1]{0:T(128)}, f32[]{:T(128)}) all-reduce(f32[9]{0:T(128)S(1)} %reshape.800, f32[1]{0:T(128)} %bitcast.59, f32[]{:T(128)} %get-tuple-element.222), channel_id=1, replica_groups=mesh['gx_0'=2,'gx_1'=4,'gy_0'=8,'gy_1'=2,'gz'=4] {'gz'}, use_global_device_ids=true, to_apply=%region_25.26 | all-reduce | flops 11 | bytes 88 | tf_op jit(solution)/shard_map/psum | solution.py:40
  392.0 2.1 collective-permute-start.16
  394.1 5.3 %collective-permute-start.17 = (f32[5,4,12,16]{3,2,1,0:T(8,128)S(1)}, f32[5,4,12,16]{3,2,1,0:T(8,128)S(1)}, u32[]{:S(2)}, u32[]{:S(2)}) collective-permute-start(f32[5,4,12,16]{3,2,1,0:T(8,128)S(1)} %pad_maximum_fusion.5), channel_id=1, source_target_pairs={{1,0},{2,1},{3,2},{0,3},{5,4},{6,5},{7,6},{4,7},{9,8},{10,9},{11,1... | collective-permute-start | bytes 46088 | tf_op jit(solution)/shard_map/ppermute | solution.py:32
  401.4 2.9 collective-permute-done.17
  406.2 3.3 gather_fusion.5
  (250 shorter events, 40.0 us)
Async XLA Ops:
  0.6 84.9 %copy-start = (f32[16,8]{0,1:T(8,128)S(1)}, f32[16,8]{0,1:T(8,128)}, u32[]{:S(2)}) copy-start(f32[16,8]{0,1:T(8,128)} %param.24) | copy-start | bytes 1540
  4.2 12.0 %collective-permute-start.1 = (f32[1,1,1,3,128]{3,4,2,1,0:T(8,128)S(1)}, f32[1,1,1,3,128]{3,4,2,1,0:T(8,128)S(1)}, u32[]{:S(2)}, u32[]{:S(2)}) collective-permute-start(f32[1,1,1,3,128]{3,4,2,1,0:T(8,128)S(1)} %bitcast_select_fusion.1), channel_id=1, source_target_pairs={{64,0},{128,64},{192,128},{256,192},{320,256},{384,320},{448,384},... | collective-permute-start | bytes 4616 | tf_op jit(solution)/shard_map/ppermute | solution.py:32
  11.3 7.1 %collective-permute-start = (f32[1,1,1,3,128]{3,4,2,1,0:T(8,128)S(1)}, f32[1,1,1,3,128]{3,4,2,1,0:T(8,128)S(1)}, u32[]{:S(2)}, u32[]{:S(2)}) collective-permute-start(f32[1,1,1,3,128]{3,4,2,1,0:T(8,128)S(1)} %bitcast_select_fusion.1), channel_id=1, source_target_pairs={{0,64},{64,128},{128,192},{192,256},{256,320},{320,384},{384,448},... | collective-permute-start | bytes 4616 | tf_op jit(solution)/shard_map/ppermute | solution.py:30
  18.5 4.1 collective-permute-start.2
  21.8 3.3 collective-permute-start.3
  25.1 11.5 %collective-permute-start.4 = (f32[3,3,1,3,128]{4,2,3,1,0:T(1,128)S(1)}, f32[3,3,1,3,128]{4,2,3,1,0:T(1,128)S(1)}, u32[]{:S(2)}, u32[]{:S(2)}) collective-permute-start(f32[3,3,1,3,128]{4,2,3,1,0:T(1,128)S(1)} %pad_maximum_fusion.12), channel_id=1, source_target_pairs={{0,1},{1,2},{2,3},{3,0},{4,5},{5,6},{6,7},{7,4},{8,9},{9,10},{10,1... | collective-permute-start | bytes 41480 | tf_op jit(solution)/shard_map/ppermute | solution.py:30
  30.6 7.4 %collective-permute-start.5 = (f32[3,3,1,3,128]{4,2,3,1,0:T(1,128)S(1)}, f32[3,3,1,3,128]{4,2,3,1,0:T(1,128)S(1)}, u32[]{:S(2)}, u32[]{:S(2)}) collective-permute-start(f32[3,3,1,3,128]{4,2,3,1,0:T(1,128)S(1)} %pad_maximum_fusion.12), channel_id=1, source_target_pairs={{1,0},{2,1},{3,2},{0,3},{5,4},{6,5},{7,6},{4,7},{9,8},{10,9},{11,1... | collective-permute-start | bytes 41480 | tf_op jit(solution)/shard_map/ppermute | solution.py:32
  39.5 41.2 %copy-start.3 = (f32[3,3968]{0,1:T(8,128)}, f32[3,3968]{0,1:T(8,128)S(1)}, u32[]{:S(2)}) copy-start(f32[3,3968]{0,1:T(8,128)S(1)} %copy.106) | copy-start | bytes 142852
  80.7 4.5 %copy-start.4 = (f32[3,512]{1,0:T(4,128)S(1)}, f32[3,512]{1,0:T(4,128)}, u32[]{:S(2)}) copy-start(f32[3,512]{1,0:T(4,128)} %param.17) | copy-start | bytes 18436
  118.0 8.1 %copy-start.11 = (f32[16]{0:T(128)S(1)}, f32[16]{0:T(128)}, u32[]{:S(2)}) copy-start(f32[16]{0:T(128)} %param.25) | copy-start | bytes 196
  124.1 2.0 copy-start.2
  141.6 12.2 %copy-start.8 = (f32[4,4,8]{2,1,0:T(4,128)S(1)}, f32[4,4,8]{2,1,0:T(4,128)}, u32[]{:S(2)}) copy-start(f32[4,4,8]{2,1,0:T(4,128)} %param.27) | copy-start | bytes 1540
  141.6 25.3 %copy-start.7 = (s32[512]{0:T(512)S(1)}, s32[512]{0:T(512)}, u32[]{:S(2)}) copy-start(s32[512]{0:T(512)} %param.23) | copy-start | bytes 6148
  141.7 29.4 %copy-start.9 = (f32[4,4,8]{2,1,0:T(4,128)S(1)}, f32[4,4,8]{2,1,0:T(4,128)}, u32[]{:S(2)}) copy-start(f32[4,4,8]{2,1,0:T(4,128)} %param.28) | copy-start | bytes 1540
  141.7 29.4 %copy-start.10 = (f32[4,4,8]{2,1,0:T(4,128)S(1)}, f32[4,4,8]{2,1,0:T(4,128)}, u32[]{:S(2)}) copy-start(f32[4,4,8]{2,1,0:T(4,128)} %param.29) | copy-start | bytes 1540
  142.7 7.4 %collective-permute-start.6 = (f32[1,1,1,128,128]{3,4,2,1,0:T(8,128)S(1)}, f32[1,1,1,128,128]{3,4,2,1,0:T(8,128)S(1)}, u32[]{:S(2)}, u32[]{:S(2)}) collective-permute-start(f32[1,1,1,128,128]{3,4,2,1,0:T(8,128)S(1)} %bitcast_select_fusion), channel_id=1, source_target_pairs={{0,64},{64,128},{128,192},{192,256},{256,320},{320,384},{384,448},... | collective-permute-start | bytes 196616 | tf_op jit(solution)/shard_map/ppermute | solution.py:30
  144.6 6.8 %collective-permute-start.7 = (f32[1,1,1,128,128]{3,4,2,1,0:T(8,128)S(1)}, f32[1,1,1,128,128]{3,4,2,1,0:T(8,128)S(1)}, u32[]{:S(2)}, u32[]{:S(2)}) collective-permute-start(f32[1,1,1,128,128]{3,4,2,1,0:T(8,128)S(1)} %bitcast_select_fusion), channel_id=1, source_target_pairs={{64,0},{128,64},{192,128},{256,192},{320,256},{384,320},{448,384},... | collective-permute-start | bytes 196616 | tf_op jit(solution)/shard_map/ppermute | solution.py:32
  151.5 5.0 %collective-permute-start.8 = (f32[3,1,1,128,128]{3,4,2,1,0:T(8,128)S(1)}, f32[3,1,1,128,128]{3,4,2,1,0:T(8,128)S(1)}, u32[]{:S(2)}, u32[]{:S(2)}) collective-permute-start(f32[3,1,1,128,128]{3,4,2,1,0:T(8,128)S(1)} %pad_maximum_fusion.4), channel_id=1, source_target_pairs={{0,4},{4,8},{8,12},{12,16},{16,20},{20,24},{24,28},{28,32},{32,36}... | collective-permute-start | bytes 589832 | tf_op jit(solution)/shard_map/ppermute | solution.py:30
  153.8 5.4 %collective-permute-start.9 = (f32[3,1,1,128,128]{3,4,2,1,0:T(8,128)S(1)}, f32[3,1,1,128,128]{3,4,2,1,0:T(8,128)S(1)}, u32[]{:S(2)}, u32[]{:S(2)}) collective-permute-start(f32[3,1,1,128,128]{3,4,2,1,0:T(8,128)S(1)} %pad_maximum_fusion.4), channel_id=1, source_target_pairs={{4,0},{8,4},{12,8},{16,12},{20,16},{24,20},{28,24},{32,28},{36,32}... | collective-permute-start | bytes 589832 | tf_op jit(solution)/shard_map/ppermute | solution.py:32
  159.2 31.1 %collective-permute-start.10 = (f32[3,3,1,128,128]{3,4,2,1,0:T(8,128)S(1)}, f32[3,3,1,128,128]{3,4,2,1,0:T(8,128)S(1)}, u32[]{:S(2)}, u32[]{:S(2)}) collective-permute-start(f32[3,3,1,128,128]{3,4,2,1,0:T(8,128)S(1)} %pad_maximum_fusion.2), channel_id=1, source_target_pairs={{0,1},{1,2},{2,3},{3,0},{4,5},{5,6},{6,7},{7,4},{8,9},{9,10},{10,1... | collective-permute-start | bytes 1769480 | tf_op jit(solution)/shard_map/ppermute | solution.py:30
  165.0 30.5 %collective-permute-start.11 = (f32[3,3,1,128,128]{3,4,2,1,0:T(8,128)S(1)}, f32[3,3,1,128,128]{3,4,2,1,0:T(8,128)S(1)}, u32[]{:S(2)}, u32[]{:S(2)}) collective-permute-start(f32[3,3,1,128,128]{3,4,2,1,0:T(8,128)S(1)} %pad_maximum_fusion.2), channel_id=1, source_target_pairs={{1,0},{2,1},{3,2},{0,3},{5,4},{6,5},{7,6},{4,7},{9,8},{10,9},{11,1... | collective-permute-start | bytes 1769480 | tf_op jit(solution)/shard_map/ppermute | solution.py:32
  195.8 66.4 %copy-start.6 = (f32[3,512]{1,0:T(4,128)S(1)}, f32[3,512]{1,0:T(4,128)}, u32[]{:S(2)}) copy-start(f32[3,512]{1,0:T(4,128)} %param.18) | copy-start | bytes 18436
  225.2 2.2 copy-start.1
  258.3 2.2 copy-start.1
  262.2 147.4 %copy-start.5 = (f32[3,512]{1,0:T(4,128)}, f32[3,512]{1,0:T(4,128)S(1)}, u32[]{:S(2)}) copy-start(f32[3,512]{1,0:T(4,128)S(1)} %get-tuple-element.170) | copy-start | bytes 18436
  266.7 34.4 %collective-permute-start.12 = (f32[5,4,4,4]{3,2,1,0:T(4,128)S(1)}, f32[5,4,4,4]{3,2,1,0:T(4,128)S(1)}, u32[]{:S(2)}, u32[]{:S(2)}) collective-permute-start(f32[5,4,4,4]{3,2,1,0:T(4,128)S(1)} %get-tuple-element.262), channel_id=1, source_target_pairs={{0,64},{64,128},{128,192},{192,256},{256,320},{320,384},{384,448},... | collective-permute-start | bytes 3848 | tf_op jit(solution)/shard_map/ppermute | solution.py:30
  298.9 4.7 %collective-permute-start.13 = (f32[5,4,4,4]{3,2,1,0:T(4,128)S(1)}, f32[5,4,4,4]{3,2,1,0:T(4,128)S(1)}, u32[]{:S(2)}, u32[]{:S(2)}) collective-permute-start(f32[5,4,4,4]{3,2,1,0:T(4,128)S(1)} %get-tuple-element.263), channel_id=1, source_target_pairs={{64,0},{128,64},{192,128},{256,192},{320,256},{384,320},{448,384},... | collective-permute-start | bytes 3848 | tf_op jit(solution)/shard_map/ppermute | solution.py:32
  303.7 88.1 %collective-permute-start.14 = (f32[5,4,4,16]{3,2,1,0:T(4,128)S(1)}, f32[5,4,4,16]{3,2,1,0:T(4,128)S(1)}, u32[]{:S(2)}, u32[]{:S(2)}) collective-permute-start(f32[5,4,4,16]{3,2,1,0:T(4,128)S(1)} %pad_maximum_fusion.11), channel_id=1, source_target_pairs={{0,4},{4,8},{8,12},{12,16},{16,20},{20,24},{24,28},{28,32},{32,36}... | collective-permute-start | bytes 15368 | tf_op jit(solution)/shard_map/ppermute | solution.py:30
  343.5 48.3 %collective-permute-start.15 = (f32[5,4,4,16]{3,2,1,0:T(4,128)S(1)}, f32[5,4,4,16]{3,2,1,0:T(4,128)S(1)}, u32[]{:S(2)}, u32[]{:S(2)}) collective-permute-start(f32[5,4,4,16]{3,2,1,0:T(4,128)S(1)} %pad_maximum_fusion.11), channel_id=1, source_target_pairs={{4,0},{8,4},{12,8},{16,12},{20,16},{24,20},{28,24},{32,28},{36,32}... | collective-permute-start | bytes 15368 | tf_op jit(solution)/shard_map/ppermute | solution.py:32
  392.0 9.4 %collective-permute-start.16 = (f32[5,4,12,16]{3,2,1,0:T(8,128)S(1)}, f32[5,4,12,16]{3,2,1,0:T(8,128)S(1)}, u32[]{:S(2)}, u32[]{:S(2)}) collective-permute-start(f32[5,4,12,16]{3,2,1,0:T(8,128)S(1)} %pad_maximum_fusion.5), channel_id=1, source_target_pairs={{0,1},{1,2},{2,3},{3,0},{4,5},{5,6},{6,7},{7,4},{8,9},{9,10},{10,1... | collective-permute-start | bytes 46088 | tf_op jit(solution)/shard_map/ppermute | solution.py:30
  394.1 10.2 %collective-permute-start.17 = (f32[5,4,12,16]{3,2,1,0:T(8,128)S(1)}, f32[5,4,12,16]{3,2,1,0:T(8,128)S(1)}, u32[]{:S(2)}, u32[]{:S(2)}) collective-permute-start(f32[5,4,12,16]{3,2,1,0:T(8,128)S(1)} %pad_maximum_fusion.5), channel_id=1, source_target_pairs={{1,0},{2,1},{3,2},{0,3},{5,4},{6,5},{7,6},{4,7},{9,8},{10,9},{11,1... | collective-permute-start | bytes 46088 | tf_op jit(solution)/shard_map/ppermute | solution.py:32
where the time goes:
time: 415 us; the launch traced here: 410 us
  local copies, waits for them, and re-layouts  141 us (34%)
  starting transfers between devices  122 us (29%)
  blocking collectives  47.6 us (11%)
  waiting for transfers between devices  41.5 us (10%)
  other arithmetic  32 us (8%)
  matrix products  22.5 us (5%)
    ppermute x9, starting transfers between devices, padded(): lax.ppermute(tail, axis, [(i, (i + 1) % count) for i in range(count)])  94.8 us
    psum x5, blocking collectives, by_axis(): return functools.reduce(lax.psum, axes, shard)  47.6 us
    gather x2, local copies, waits for them, and re-layouts, local(): separation = pos_table[:, neighbour_index] - positions[:, None, :]  45.6 us
    gather x4, local copies, waits for them, and re-layouts, one_block(): block_sep = pos_table[:, index_block] - own_block[:, None, :]  28.6 us
    gather x4, local copies, waits for them, and re-layouts, one_block(): adjoint_table[:, index_block].reshape(orders, 16, neigh_depth, block_rows)  27.7 us
    ppermute x9, starting transfers between devices, padded(): lax.ppermute(head, axis, [((i + 1) % count, i) for i in range(count)])  27.5 us
    ppermute x9, waiting for transfers between devices, padded(): lax.ppermute(tail, axis, [(i, (i + 1) % count) for i in range(count)])  22.9 us
    ppermute x9, waiting for transfers between devices, padded(): lax.ppermute(head, axis, [((i + 1) % count, i) for i in range(count)])  18.6 us
  transfers between devices with their start and end apart: 18, of which 11 were waited for; matrix products, arithmetic and copies ran while one was open for 3% of the time, Pallas kernels for 0%

commit v1 on v0

--- a/solution.py
+++ b/solution.py
@@ -38,6 +38,23 @@
 
 def by_axis(shard, axes):
     return functools.reduce(lax.psum, axes, shard)
+
+
+def column_gather(table, index):
+    rows, width = table.shape
+    lanes = 128
+    blocks = -(-width // lanes)
+    padded_table = jnp.pad(table, ((0, 0), (0, blocks * lanes - width)))
+    flat = index.reshape(-1)
+    high = flat // lanes
+    low = flat % lanes
+    picks = (jnp.arange(lanes)[:, None] == low[None, :]).astype(jnp.float32)
+    spread = jnp.dot(
+        padded_table.reshape(rows * blocks, lanes), picks, precision=lax.Precision.HIGHEST
+    ).reshape(rows, blocks, flat.shape[0])
+    chosen = jnp.arange(blocks)[:, None] == high[None, :]
+    gathered = jnp.sum(jnp.where(chosen[None], spread, 0.0), axis=1)
+    return gathered.reshape((rows,) + index.shape)
 
 
 def harmonics(vector):
@@ -105,7 +122,8 @@
     energy = jnp.dot(linear_weight, basis_sum[:, 0, :], precision=lax.Precision.HIGHEST) + jnp.sum(
         basis_sum * forward, axis=(0, 1)
     )
-    adjoint = (forward + backward).at[:, 0, :].add(linear_weight[:, None])
+    isotropic = (jnp.arange(basis_sum.shape[1]) == 0).astype(jnp.float32)
+    adjoint = forward + backward + linear_weight[:, None, None] * isotropic[None, :, None]
     return (energy, adjoint)
 
 
@@ -170,7 +188,7 @@
     pos_table = jnp.concatenate(
         [positions, jnp.transpose(shifted, (1, 0, 2)).reshape(3, 27 * ghosts)], axis=1
     )
-    separation = pos_table[:, neighbour_index] - positions[:, None, :]
+    separation = column_gather(pos_table, neighbour_index) - positions[:, None, :]
     pair_mask = (jnp.arange(neigh_depth)[:, None] < neighbour_count[None, :]).astype(jnp.float32)
     basis_sum = atom_basis(separation, pair_mask, radial_weight)
     energy, adjoint = adjoints(basis_sum, linear_weight, pair_coupling)
@@ -182,30 +200,11 @@
     adjoint_table = jnp.concatenate(
         [own_table, jnp.transpose(remote, (1, 0, 2)).reshape(orders * 16, 27 * ghosts)], axis=1
     )
-    block_rows = 128
-    live_blocks = (live_count + block_rows - 1) // block_rows
-
-    def one_block(block_id, carry):
-        forces_acc, virial_acc = carry
-        start = block_id * block_rows
-        index_block = lax.dynamic_slice_in_dim(neighbour_index, start, block_rows, 1)
-        count_block = lax.dynamic_slice_in_dim(neighbour_count, start, block_rows, 0)
-        own_block = lax.dynamic_slice_in_dim(positions, start, block_rows, 1)
-        weights_block = lax.dynamic_slice_in_dim(own_table, start, block_rows, 1)
-        block_sep = pos_table[:, index_block] - own_block[:, None, :]
-        block_mask = (jnp.arange(neigh_depth)[:, None] < count_block[None, :]).astype(jnp.float32)
-        other_weights = adjoint_table[:, index_block].reshape(orders, 16, neigh_depth, block_rows)
-        block_force, block_virial = pair_forces(
-            block_sep, block_mask, weights_block.reshape(orders, 16, 1, block_rows), other_weights
-        )
-        forces_acc = lax.dynamic_update_slice_in_dim(forces_acc, block_force, start, 1)
-        return (forces_acc, virial_acc + block_virial)
-
-    forces, virial = lax.fori_loop(
-        0,
-        live_blocks,
-        one_block,
-        (jnp.zeros((3, atom_slots), jnp.float32), jnp.zeros((3, 3), jnp.float32)),
+    other_weights = adjoint_table[:, neighbour_index].reshape(
+        orders, 16, neigh_depth, atom_slots
+    )
+    forces, virial = pair_forces(
+        separation, pair_mask, own_table.reshape(orders, 16, 1, atom_slots), other_weights
     )
     kicked = velocities + KICK * forces
     grid_shape = electron_temp.shape
@@ -247,14 +246,15 @@
     exchange_rate = RELAX * (electron - lattice) / (electron + lattice)
     scaling = jnp.take(exchange_rate.reshape(-1), atom_cell)
     new_velocity = kicked * (1.0 + scaling) * alive_mask
-    count_total, energy_total, virial_total = (
-        by_axis(live_count.astype(jnp.float32), GX_GY_GZ),
-        by_axis(jnp.sum(energy * alive_mask), GX_GY_GZ),
-        by_axis(virial, GX_GY_GZ),
-    )
-    totals = (
-        jnp.concatenate([jnp.reshape(energy_total, (1,)), virial_total.reshape(9)]) / count_total
-    )
+    packed = jnp.concatenate(
+        [
+            jnp.reshape(jnp.sum(energy * alive_mask), (1,)),
+            virial.reshape(9),
+            jnp.reshape(live_count.astype(jnp.float32), (1,)),
+        ]
+    )
+    summed = lax.psum(packed, GX_GY_GZ)
+    totals = summed[:10] / summed[10]
     return (forces, new_velocity, electron, totals)
 
 

time: 415 us -> 340 us (0.82); the launches traced: 410 us -> 339 us
  local copies, waits for them, and re-layouts: 141 us -> 78.3 us
  starting transfers between devices: 122 us -> 61.1 us
  blocking collectives: 47.6 us -> 99.4 us
    ppermute x9, starting transfers between devices: 94.8 us -> 14.1 us  [padded(): lax.ppermute(tail, axis, [(i, (i + 1) % count) for i in range(count)])]
    gather x10 -> x2, local copies, waits for them, and re-layouts: 102 us -> 48 us  [local(): adjoint_table[:, neighbour_index]]
    psum x5 -> x1, blocking collectives: 47.6 us -> 99.4 us  [local(): summed = lax.psum(packed, GX_GY_GZ)]
    ppermute x9, starting transfers between devices: 27.5 us -> 47 us  [padded(): lax.ppermute(head, axis, [((i + 1) % count, i) for i in range(count)])]
    scatter-add x1 -> x0, local copies, waits for them, and re-layouts: 8.25 us -> none  [adjoints(): adjoint = (forward + backward).at[:, 0, :].add(linear_weight[:, None])]
    ppermute x9, waiting for transfers between devices: 22.9 us -> 16.2 us  [padded(): lax.ppermute(tail, axis, [(i, (i + 1) % count) for i in range(count)])]
    ppermute x9, waiting for transfers between devices: 18.6 us -> 24.2 us  [padded(): lax.ppermute(head, axis, [((i + 1) % count, i) for i in range(count)])]
  transfers between devices with their start and end apart: 18 -> 18, of which waited for: 11 -> 11; matrix products, arithmetic and copies ran while one was open for 3% -> 4% of each run, Pallas kernels for 0% -> 0%
where the time goes in v1:
time: 340 us; the launch traced here: 339 us
  blocking collectives  99.4 us (29%)
  local copies, waits for them, and re-layouts  78.3 us (23%)
  starting transfers between devices  61.1 us (18%)
  waiting for transfers between devices  40.4 us (12%)
  other arithmetic  33.9 us (10%)
  matrix products  24.1 us (7%)
    psum x1, blocking collectives, local(): summed = lax.psum(packed, GX_GY_GZ)  99.4 us
    gather x2, local copies, waits for them, and re-layouts, local(): adjoint_table[:, neighbour_index]  48 us
    ppermute x9, starting transfers between devices, padded(): lax.ppermute(head, axis, [((i + 1) % count, i) for i in range(count)])  47 us
    ppermute x9, waiting for transfers between devices, padded(): lax.ppermute(head, axis, [((i + 1) % count, i) for i in range(count)])  24.2 us
    ppermute x9, waiting for transfers between devices, padded(): lax.ppermute(tail, axis, [(i, (i + 1) % count) for i in range(count)])  16.2 us
    ppermute x9, starting transfers between devices, padded(): lax.ppermute(tail, axis, [(i, (i + 1) % count) for i in range(count)])  14.1 us
    dot_general x1, matrix products, atom_basis(): jnp.einsum('nka,mka->nma', shaped, harmonics(separation), precision=lax.P...  12.2 us
  transfers between devices with their start and end apart: 18, of which 11 were waited for; matrix products, arithmetic and copies ran while one was open for 4% of the time, Pallas kernels for 0%

profile of v1, /device:TPU:1, one launch (start us, length us, event | category | flops | bytes accessed | tf_op | source)
XLA Modules:
  0.0 339.4 jit_solution(17959087077124072818)
XLA Ops:
  2.7 0.8 copy.123
  4.3 7.0 %collective-permute-start.1 = (f32[1,1,1,3,128]{3,4,2,1,0:T(8,128)S(1)}, f32[1,1,1,3,128]{3,4,2,1,0:T(8,128)S(1)}, u32[]{:S(2)}, u32[]{:S(2)}) collective-permute-start(f32[1,1,1,3,128]{3,4,2,1,0:T(8,128)S(1)} %bitcast_select_fusion.1), channel_id=1, source_target_pairs={{64,0},{128,64},{192,128},{256,192},{320,256},{384,320},{448,384},... | collective-permute-start | bytes 4616 | tf_op jit(solution)/shard_map/ppermute | solution.py:32
  11.3 1.9 collective-permute-start
  16.7 0.8 fusion.122
  17.5 0.8 copy.152
  19.6 3.8 %collective-permute-start.3 = (f32[3,1,1,3,128]{4,2,3,1,0:T(1,128)S(1)}, f32[3,1,1,3,128]{4,2,3,1,0:T(1,128)S(1)}, u32[]{:S(2)}, u32[]{:S(2)}) collective-permute-start(f32[3,1,1,3,128]{4,2,3,1,0:T(1,128)S(1)} %pad_maximum_fusion.13), channel_id=1, source_target_pairs={{4,0},{8,4},{12,8},{16,12},{20,16},{24,20},{28,24},{32,28},{36,32}... | collective-permute-start | bytes 13832 | tf_op jit(solution)/shard_map/ppermute | solution.py:32
  23.4 0.8 collective-permute-done.3
  24.6 9.1 %collective-permute-start.5 = (f32[3,3,1,3,128]{4,2,3,1,0:T(1,128)S(1)}, f32[3,3,1,3,128]{4,2,3,1,0:T(1,128)S(1)}, u32[]{:S(2)}, u32[]{:S(2)}) collective-permute-start(f32[3,3,1,3,128]{4,2,3,1,0:T(1,128)S(1)} %pad_maximum_fusion.12), channel_id=1, source_target_pairs={{1,0},{2,1},{3,2},{0,3},{5,4},{6,5},{7,6},{4,7},{9,8},{10,9},{11,1... | collective-permute-start | bytes 41480 | tf_op jit(solution)/shard_map/ppermute | solution.py:32
  33.6 1.9 collective-permute-start.4
  35.7 4.5 %collective-permute-done.4 = f32[3,3,1,3,128]{4,2,3,1,0:T(1,128)S(1)} collective-permute-done((f32[3,3,1,3,128]{4,2,3,1,0:T(1,128)S(1)}, f32[3,3,1,3,128]{4,2,3,1,0:T(1,128)S(1)}, u32[]{:S(2)}, u32[]{:S(2)}) %collective-permute-start.4) | collective-permute-done | bytes 13856 | tf_op jit(solution)/shard_map/ppermute | solution.py:30
  41.1 3.4 fusion.7
  46.6 1.0 fusion.10
  47.6 3.8 %copy.133 = f32[16,24,512]{1,0,2:T(8,128)} copy(f32[16,24,512]{2,0,1:T(8,128)S(1)} %fusion.10) | data formatting | bytes 1572864 | tf_op jit(solution)/shard_map/mul | solution.py:105
  51.4 3.7 %copy.132 = f32[16,24,512]{1,0,2:T(8,128)} copy(f32[16,24,512]{2,1,0:T(8,128)S(1)} %constant_dynamic-update-slice_fusion) | data formatting | bytes 1572864 | tf_op jit(solution)/shard_map/stack | solution.py:83
  55.0 12.2 %fusion.275 = f32[512,16,16]{2,1,0:T(8,128)} fusion(f32[16,24,512]{1,0,2:T(8,128)} %copy.132, f32[16,24,512]{1,0,2:T(8,128)} %copy.133), kind=kOutput, calls=%fused_computation.581 | convolution fusion | flops 37748736 | bytes 2097152 | tf_op jit(solution)/shard_map/nka,mka->nma/dot_general | solution.py:107
  67.2 2.8 copy.134
  71.3 3.7 %copy.135 = f32[16,512,16]{2,0,1:T(8,128)} copy(f32[16,512,16]{1,2,0:T(8,128)S(1)} %fusion.20) | data formatting | bytes 1048576 | tf_op jit(solution)/shard_map/mnp,pma->nma/dot_general | solution.py:120
  74.9 3.6 %copy.138 = f32[16,512,16]{2,0,1:T(8,128)} copy(f32[16,512,16]{1,2,0:T(8,128)S(1)} %fusion.19) | data formatting | bytes 1048576 | tf_op jit(solution)/shard_map/mpn,pma->nma/dot_general | solution.py:121
  78.6 6.2 %fusion.3 = (f32[512]{0:T(512)S(1)}, f32[16,16,512]{0,1,2:T(8,128)S(1)}) fusion(f32[16,512,16]{2,0,1:T(8,128)} %copy.135, f32[512,16,16]{2,1,0:T(8,128)} %fusion.275, f32[16,16]{0,1:T(8,128)S(1)} %broadcast_multiply_fusion.3, f32[16,512,16]{2,0,1:T(8,128)} %copy.138), kind=kLoop, calls=%fused_computation.16 | loop fusion | flops 523776 | bytes 2100224 | tf_op jit(solution)/shard_map/reduce_sum | solution.py:122
  84.8 5.0 %fusion.11 = f32[8,16,512]{2,0,1:T(8,128)S(1)} fusion(f32[16,16,512]{0,1,2:T(8,128)S(1)} %get-tuple-element.30, f32[16,8]{0,1:T(8,128)S(1)} %copy-done), kind=kOutput, calls=%fused_computation.26 | convolution fusion | flops 12582912 | bytes 786944 | tf_op jit(solution)/shard_map/nc,nma->cma/dot_general | solution.py:195
  90.9 5.6 %collective-permute-start.7 = (f32[1,1,1,128,128]{3,4,2,1,0:T(8,128)S(1)}, f32[1,1,1,128,128]{3,4,2,1,0:T(8,128)S(1)}, u32[]{:S(2)}, u32[]{:S(2)}) collective-permute-start(f32[1,1,1,128,128]{3,4,2,1,0:T(8,128)S(1)} %bitcast_select_fusion), channel_id=1, source_target_pairs={{64,0},{128,64},{192,128},{256,192},{320,256},{384,320},{448,384},... | collective-permute-start | bytes 196616 | tf_op jit(solution)/shard_map/ppermute | solution.py:32
  96.5 1.9 collective-permute-start.6
  98.4 5.2 %collective-permute-done.6 = f32[1,1,1,128,128]{3,4,2,1,0:T(8,128)S(1)} collective-permute-done((f32[1,1,1,128,128]{3,4,2,1,0:T(8,128)S(1)}, f32[1,1,1,128,128]{3,4,2,1,0:T(8,128)S(1)}, u32[]{:S(2)}, u32[]{:S(2)}) %collective-permute-start.6) | collective-permute-done | bytes 65568 | tf_op jit(solution)/shard_map/ppermute | solution.py:30
  103.6 6.5 %collective-permute-start.9 = (f32[3,1,1,128,128]{3,4,2,1,0:T(8,128)S(1)}, f32[3,1,1,128,128]{3,4,2,1,0:T(8,128)S(1)}, u32[]{:S(2)}, u32[]{:S(2)}) collective-permute-start(f32[3,1,1,128,128]{3,4,2,1,0:T(8,128)S(1)} %pad_maximum_fusion.4), channel_id=1, source_target_pairs={{4,0},{8,4},{12,8},{16,12},{20,16},{24,20},{28,24},{32,28},{36,32}... | collective-permute-start | bytes 589832 | tf_op jit(solution)/shard_map/ppermute | solution.py:32
  110.1 1.1 collective-permute-done.9
  111.1 1.5 collective-permute-done.8
  112.7 0.9 pad_maximum_fusion.2
  113.5 1.9 collective-permute-start.11
  115.5 4.3 %collective-permute-start.10 = (f32[3,3,1,128,128]{3,4,2,1,0:T(8,128)}, f32[3,3,1,128,128]{3,4,2,1,0:T(8,128)S(1)}, u32[]{:S(2)}, u32[]{:S(2)}) collective-permute-start(f32[3,3,1,128,128]{3,4,2,1,0:T(8,128)} %pad_maximum_fusion.2), channel_id=1, source_target_pairs={{0,1},{1,2},{2,3},{3,0},{4,5},{5,6},{6,7},{7,4},{8,9},{9,10},{10,1... | collective-permute-start | bytes 1769480 | tf_op jit(solution)/shard_map/ppermute | solution.py:30
  119.8 4.1 %scatter_custom_fusion.1 = f32[128]{0:T(128)S(1)} fusion(s32[512]{0:T(512)S(1)} %copy-done.9, f32[512]{0:T(512)S(1)} %fusion.251, f32[]{:T(128)} %constant.156.clone.1), kind=kCustom, calls=%fused_computation.570 | custom fusion | flops 512 | bytes 516 | tf_op jit(solution)/shard_map/scatter-add | solution.py:215
  123.9 1.7 slice.481
  126.6 17.3 %collective-permute-done.11 = f32[3,3,1,128,128]{3,4,2,1,0:T(8,128)S(1)} collective-permute-done((f32[3,3,1,128,128]{3,4,2,1,0:T(8,128)}, f32[3,3,1,128,128]{3,4,2,1,0:T(8,128)S(1)}, u32[]{:S(2)}, u32[]{:S(2)}) %collective-permute-start.11) | collective-permute-done | bytes 589856 | tf_op jit(solution)/shard_map/ppermute | solution.py:32
  144.8 41.3 %gather_fusion.2 = f32[12288,128]{1,0:T(8,128)} fusion(f32[128,3968]{0,1:T(8,128)S(1)} %pad_maximum_fusion, s32[12288]{0:T(1024)S(1)} %broadcast_clamp_fusion), kind=kCustom, calls=%fused_computation.2 | custom fusion | bytes 12632064 | tf_op jit(solution)/shard_map/gather | solution.py:203
  186.1 6.8 %copy.144 = f32[24,512,128]{1,0,2:T(8,128)} copy(f32[24,512,128]{2,1,0:T(8,128)} %bitcast.281) | data formatting | bytes 12582912 | tf_op jit(solution)/shard_map/gather | solution.py:203
  192.9 4.1 %multiply_reduce_fusion.3 = (f32[16,24,512]{2,1,0:T(8,128)S(1)}, f32[16,24,512]{2,1,0:T(8,128)S(1)}, f32[8,24,512]{2,1,0:T(8,128)S(1)}) fusion(f32[8,24,512]{2,1,0:T(8,128)S(1)} %broadcast_multiply_fusion.2, f32[8,16,512]{2,1,0:T(8,128)S(1)} %copy.140, f32[8,16,24,512]{3,2,1,0:T(8,128)} %bitcast.277, f32[16,24,512]{2,1,0:T(8,128)S(1)} %copy-done.2), kind=kLoop, calls=%fused_computation.10 | loop fusion | flops 8945664 | bytes 9699328 | tf_op jit(solution)/shard_map/jvp()/reduce_sum | solution.py:98
  198.0 0.9 multiply_reduce_fusion
  199.4 1.0 convolution_bitcast_fusion
  200.5 4.1 %scatter_custom_fusion = f32[128]{0:T(128)S(1)} fusion(s32[512]{0:T(512)S(1)} %copy-done.9, f32[512]{0:T(512)S(1)} %fusion.252, f32[]{:T(128)} %constant.156.clone.1), kind=kCustom, calls=%fused_computation.572 | custom fusion | flops 512 | bytes 516 | tf_op jit(solution)/shard_map/scatter-add | solution.py:212
  205.0 1.9 collective-permute-start.12
  206.9 5.5 %collective-permute-start.13 = (f32[5,4,4,4]{3,2,1,0:T(4,128)S(1)}, f32[5,4,4,4]{3,2,1,0:T(4,128)S(1)}, u32[]{:S(2)}, u32[]{:S(2)}) collective-permute-start(f32[5,4,4,4]{3,2,1,0:T(4,128)S(1)} %get-tuple-element.52), channel_id=1, source_target_pairs={{64,0},{128,64},{192,128},{256,192},{320,256},{384,320},{448,384},... | collective-permute-start | bytes 3848 | tf_op jit(solution)/shard_map/ppermute | solution.py:32
  213.6 3.7 %collective-permute-start.15 = (f32[5,4,4,16]{3,2,1,0:T(4,128)S(1)}, f32[5,4,4,16]{3,2,1,0:T(4,128)S(1)}, u32[]{:S(2)}, u32[]{:S(2)}) collective-permute-start(f32[5,4,4,16]{3,2,1,0:T(4,128)S(1)} %pad_maximum_fusion.11), channel_id=1, source_target_pairs={{4,0},{8,4},{12,8},{16,12},{20,16},{24,20},{28,24},{32,28},{36,32}... | collective-permute-start | bytes 15368 | tf_op jit(solution)/shard_map/ppermute | solution.py:32
  217.2 99.4 %psum.7 = f32[11]{0:T(128)S(1)} all-reduce(f32[11]{0:T(128)S(1)} %pad_maximum_fusion.14), channel_id=1, replica_groups=mesh['gx_0'=2,'gx_1'=4,'gy_0'=8,'gy_1'=2,'gz'=4] {'gx_0','gx_1','gy_0','..., use_global_device_ids=true, to_apply=%region_14.15 | all-reduce | flops 11 | bytes 88 | tf_op jit(solution)/shard_map/psum | solution.py:256
  317.4 4.0 %collective-permute-start.17 = (f32[5,4,12,16]{3,2,1,0:T(8,128)S(1)}, f32[5,4,12,16]{3,2,1,0:T(8,128)S(1)}, u32[]{:S(2)}, u32[]{:S(2)}) collective-permute-start(f32[5,4,12,16]{3,2,1,0:T(8,128)S(1)} %pad_maximum_fusion.5), channel_id=1, source_target_pairs={{1,0},{2,1},{3,2},{0,3},{5,4},{6,5},{7,6},{4,7},{9,8},{10,9},{11,1... | collective-permute-start | bytes 46088 | tf_op jit(solution)/shard_map/ppermute | solution.py:32
  321.4 2.2 collective-permute-start.16
  323.6 1.2 slice_divide_fusion
  324.8 4.6 %collective-permute-done.17 = f32[5,4,12,16]{3,2,1,0:T(8,128)S(1)} collective-permute-done((f32[5,4,12,16]{3,2,1,0:T(8,128)S(1)}, f32[5,4,12,16]{3,2,1,0:T(8,128)S(1)}, u32[]{:S(2)}, u32[]{:S(2)}) %collective-permute-start.17) | collective-permute-done | bytes 15392 | tf_op jit(solution)/shard_map/ppermute | solution.py:32
  329.5 4.0 %collective-permute-done.16 = f32[5,4,12,16]{3,2,1,0:T(8,128)S(1)} collective-permute-done((f32[5,4,12,16]{3,2,1,0:T(8,128)S(1)}, f32[5,4,12,16]{3,2,1,0:T(8,128)S(1)}, u32[]{:S(2)}, u32[]{:S(2)}) %collective-permute-start.16) | collective-permute-done | bytes 15392 | tf_op jit(solution)/shard_map/ppermute | solution.py:30
  335.4 3.3 gather_fusion.3
  (164 shorter events, 20.6 us)
Async XLA Ops:
  0.6 46.0 %copy-start = (f32[16,8]{0,1:T(8,128)S(1)}, f32[16,8]{0,1:T(8,128)}, u32[]{:S(2)}) copy-start(f32[16,8]{0,1:T(8,128)} %param.20) | copy-start | bytes 1540
  0.6 43.8 %copy-start.6 = (f32[3,512]{1,0:T(4,128)S(1)}, f32[3,512]{1,0:T(4,128)}, u32[]{:S(2)}) copy-start(f32[3,512]{1,0:T(4,128)} %param.13) | copy-start | bytes 18436
  4.3 15.2 %collective-permute-start.1 = (f32[1,1,1,3,128]{3,4,2,1,0:T(8,128)S(1)}, f32[1,1,1,3,128]{3,4,2,1,0:T(8,128)S(1)}, u32[]{:S(2)}, u32[]{:S(2)}) collective-permute-start(f32[1,1,1,3,128]{3,4,2,1,0:T(8,128)S(1)} %bitcast_select_fusion.1), channel_id=1, source_target_pairs={{64,0},{128,64},{192,128},{256,192},{320,256},{384,320},{448,384},... | collective-permute-start | bytes 4616 | tf_op jit(solution)/shard_map/ppermute | solution.py:32
  11.3 8.2 %collective-permute-start = (f32[1,1,1,3,128]{3,4,2,1,0:T(8,128)S(1)}, f32[1,1,1,3,128]{3,4,2,1,0:T(8,128)S(1)}, u32[]{:S(2)}, u32[]{:S(2)}) collective-permute-start(f32[1,1,1,3,128]{3,4,2,1,0:T(8,128)S(1)} %bitcast_select_fusion.1), channel_id=1, source_target_pairs={{0,64},{64,128},{128,192},{192,256},{256,320},{320,384},{384,448},... | collective-permute-start | bytes 4616 | tf_op jit(solution)/shard_map/ppermute | solution.py:30
  19.6 4.6 %collective-permute-start.3 = (f32[3,1,1,3,128]{4,2,3,1,0:T(1,128)S(1)}, f32[3,1,1,3,128]{4,2,3,1,0:T(1,128)S(1)}, u32[]{:S(2)}, u32[]{:S(2)}) collective-permute-start(f32[3,1,1,3,128]{4,2,3,1,0:T(1,128)S(1)} %pad_maximum_fusion.13), channel_id=1, source_target_pairs={{4,0},{8,4},{12,8},{16,12},{20,16},{24,20},{28,24},{32,28},{36,32}... | collective-permute-start | bytes 13832 | tf_op jit(solution)/shard_map/ppermute | solution.py:32
  23.4 1.2 collective-permute-start.2
  24.6 11.1 %collective-permute-start.5 = (f32[3,3,1,3,128]{4,2,3,1,0:T(1,128)S(1)}, f32[3,3,1,3,128]{4,2,3,1,0:T(1,128)S(1)}, u32[]{:S(2)}, u32[]{:S(2)}) collective-permute-start(f32[3,3,1,3,128]{4,2,3,1,0:T(1,128)S(1)} %pad_maximum_fusion.12), channel_id=1, source_target_pairs={{1,0},{2,1},{3,2},{0,3},{5,4},{6,5},{7,6},{4,7},{9,8},{10,9},{11,1... | collective-permute-start | bytes 41480 | tf_op jit(solution)/shard_map/ppermute | solution.py:32
  33.6 6.6 %collective-permute-start.4 = (f32[3,3,1,3,128]{4,2,3,1,0:T(1,128)S(1)}, f32[3,3,1,3,128]{4,2,3,1,0:T(1,128)S(1)}, u32[]{:S(2)}, u32[]{:S(2)}) collective-permute-start(f32[3,3,1,3,128]{4,2,3,1,0:T(1,128)S(1)} %pad_maximum_fusion.12), channel_id=1, source_target_pairs={{0,1},{1,2},{2,3},{3,0},{4,5},{5,6},{6,7},{7,4},{8,9},{9,10},{10,1... | collective-permute-start | bytes 41480 | tf_op jit(solution)/shard_map/ppermute | solution.py:30
  45.5 9.5 %copy-start.1 = (f32[16,24,512]{2,1,0:T(8,128)}, f32[16,24,512]{2,1,0:T(8,128)S(1)}, u32[]{:S(2)}) copy-start(f32[16,24,512]{2,1,0:T(8,128)S(1)} %constant_dynamic-update-slice_fusion) | copy-start | bytes 2359300
  45.8 0.8 copy-start.3
  84.8 25.3 %copy-start.10 = (f32[4,4,8]{2,1,0:T(4,128)S(1)}, f32[4,4,8]{2,1,0:T(4,128)}, u32[]{:S(2)}) copy-start(f32[4,4,8]{2,1,0:T(4,128)} %param.24) | copy-start | bytes 1540
  84.8 35.0 %copy-start.9 = (s32[512]{0:T(512)S(1)}, s32[512]{0:T(512)}, u32[]{:S(2)}) copy-start(s32[512]{0:T(512)} %param.19) | copy-start | bytes 6148
  84.8 39.0 %copy-start.11 = (f32[4,4,8]{2,1,0:T(4,128)S(1)}, f32[4,4,8]{2,1,0:T(4,128)}, u32[]{:S(2)}) copy-start(f32[4,4,8]{2,1,0:T(4,128)} %param.25) | copy-start | bytes 1540
  84.8 40.8 %copy-start.12 = (f32[16]{0:T(128)S(1)}, f32[16]{0:T(128)}, u32[]{:S(2)}) copy-start(f32[16]{0:T(128)} %param.21) | copy-start | bytes 196
  90.9 7.6 %collective-permute-start.7 = (f32[1,1,1,128,128]{3,4,2,1,0:T(8,128)S(1)}, f32[1,1,1,128,128]{3,4,2,1,0:T(8,128)S(1)}, u32[]{:S(2)}, u32[]{:S(2)}) collective-permute-start(f32[1,1,1,128,128]{3,4,2,1,0:T(8,128)S(1)} %bitcast_select_fusion), channel_id=1, source_target_pairs={{64,0},{128,64},{192,128},{256,192},{320,256},{384,320},{448,384},... | collective-permute-start | bytes 196616 | tf_op jit(solution)/shard_map/ppermute | solution.py:32
  96.5 7.1 %collective-permute-start.6 = (f32[1,1,1,128,128]{3,4,2,1,0:T(8,128)S(1)}, f32[1,1,1,128,128]{3,4,2,1,0:T(8,128)S(1)}, u32[]{:S(2)}, u32[]{:S(2)}) collective-permute-start(f32[1,1,1,128,128]{3,4,2,1,0:T(8,128)S(1)} %bitcast_select_fusion), channel_id=1, source_target_pairs={{0,64},{64,128},{128,192},{192,256},{256,320},{320,384},{384,448},... | collective-permute-start | bytes 196616 | tf_op jit(solution)/shard_map/ppermute | solution.py:30
  103.6 7.5 %collective-permute-start.9 = (f32[3,1,1,128,128]{3,4,2,1,0:T(8,128)S(1)}, f32[3,1,1,128,128]{3,4,2,1,0:T(8,128)S(1)}, u32[]{:S(2)}, u32[]{:S(2)}) collective-permute-start(f32[3,1,1,128,128]{3,4,2,1,0:T(8,128)S(1)} %pad_maximum_fusion.4), channel_id=1, source_target_pairs={{4,0},{8,4},{12,8},{16,12},{20,16},{24,20},{28,24},{32,28},{36,32}... | collective-permute-start | bytes 589832 | tf_op jit(solution)/shard_map/ppermute | solution.py:32
  110.1 2.6 collective-permute-start.8
  113.5 30.3 %collective-permute-start.11 = (f32[3,3,1,128,128]{3,4,2,1,0:T(8,128)}, f32[3,3,1,128,128]{3,4,2,1,0:T(8,128)S(1)}, u32[]{:S(2)}, u32[]{:S(2)}) collective-permute-start(f32[3,3,1,128,128]{3,4,2,1,0:T(8,128)} %pad_maximum_fusion.2), channel_id=1, source_target_pairs={{1,0},{2,1},{3,2},{0,3},{5,4},{6,5},{7,6},{4,7},{9,8},{10,9},{11,1... | collective-permute-start | bytes 1769480 | tf_op jit(solution)/shard_map/ppermute | solution.py:32
  115.5 29.1 %collective-permute-start.10 = (f32[3,3,1,128,128]{3,4,2,1,0:T(8,128)}, f32[3,3,1,128,128]{3,4,2,1,0:T(8,128)S(1)}, u32[]{:S(2)}, u32[]{:S(2)}) collective-permute-start(f32[3,3,1,128,128]{3,4,2,1,0:T(8,128)} %pad_maximum_fusion.2), channel_id=1, source_target_pairs={{0,1},{1,2},{2,3},{3,0},{4,5},{5,6},{6,7},{7,4},{8,9},{9,10},{10,1... | collective-permute-start | bytes 1769480 | tf_op jit(solution)/shard_map/ppermute | solution.py:30
  186.1 6.8 %copy-start.2 = (f32[16,24,512]{2,1,0:T(8,128)S(1)}, f32[16,24,512]{2,1,0:T(8,128)}, u32[]{:S(2)}) copy-start(f32[16,24,512]{2,1,0:T(8,128)} %copy-done.1) | copy-start | bytes 2359300
  192.9 5.1 %slice-start = ((s8[6291456]{0:T(1024)(128)(4,1)}), s8[4194304]{0:T(1024)(128)(4,1)S(1)}, s32[]{:S(2)}) async-start(s8[6291456]{0:T(1024)(128)(4,1)} %bitcast.278), calls=%async_computation | async-start | bytes 8388608
  192.9 4.5 %copy-start.5 = (f32[16,24,512]{2,1,0:T(8,128)S(1)}, f32[16,24,512]{2,1,0:T(8,128)}, u32[]{:S(2)}) copy-start(f32[16,24,512]{2,1,0:T(8,128)} %get-tuple-element.27) | copy-start | bytes 2359300
  192.9 5.1 %slice-start.1 = ((s8[6291456]{0:T(1024)(128)(4,1)}), s8[2097152]{0:T(1024)(128)(4,1)S(1)}, s32[]{:S(2)}) async-start(s8[6291456]{0:T(1024)(128)(4,1)} %bitcast.278), calls=%async_computation.1 | async-start | bytes 4194304
  197.9 1.0 copy-start.4
  198.0 2.5 copy-start.8
  199.4 139.4 %copy-start.7 = (f32[3,512]{1,0:T(4,128)}, f32[3,512]{1,0:T(4,128)S(1)}, u32[]{:S(2)}) copy-start(f32[3,512]{1,0:T(4,128)S(1)} %get-tuple-element.25) | copy-start | bytes 18436
  205.0 8.1 %collective-permute-start.12 = (f32[5,4,4,4]{3,2,1,0:T(4,128)S(1)}, f32[5,4,4,4]{3,2,1,0:T(4,128)S(1)}, u32[]{:S(2)}, u32[]{:S(2)}) collective-permute-start(f32[5,4,4,4]{3,2,1,0:T(4,128)S(1)} %get-tuple-element.51), channel_id=1, source_target_pairs={{0,64},{64,128},{128,192},{192,256},{256,320},{320,384},{384,448},... | collective-permute-start | bytes 3848 | tf_op jit(solution)/shard_map/ppermute | solution.py:30
  206.9 6.6 %collective-permute-start.13 = (f32[5,4,4,4]{3,2,1,0:T(4,128)S(1)}, f32[5,4,4,4]{3,2,1,0:T(4,128)S(1)}, u32[]{:S(2)}, u32[]{:S(2)}) collective-permute-start(f32[5,4,4,4]{3,2,1,0:T(4,128)S(1)} %get-tuple-element.52), channel_id=1, source_target_pairs={{64,0},{128,64},{192,128},{256,192},{320,256},{384,320},{448,384},... | collective-permute-start | bytes 3848 | tf_op jit(solution)/shard_map/ppermute | solution.py:32
  213.6 103.7 %collective-permute-start.15 = (f32[5,4,4,16]{3,2,1,0:T(4,128)S(1)}, f32[5,4,4,16]{3,2,1,0:T(4,128)S(1)}, u32[]{:S(2)}, u32[]{:S(2)}) collective-permute-start(f32[5,4,4,16]{3,2,1,0:T(4,128)S(1)} %pad_maximum_fusion.11), channel_id=1, source_target_pairs={{4,0},{8,4},{12,8},{16,12},{20,16},{24,20},{28,24},{32,28},{36,32}... | collective-permute-start | bytes 15368 | tf_op jit(solution)/shard_map/ppermute | solution.py:32
  217.2 100.0 %collective-permute-start.14 = (f32[5,4,4,16]{3,2,1,0:T(4,128)S(1)}, f32[5,4,4,16]{3,2,1,0:T(4,128)S(1)}, u32[]{:S(2)}, u32[]{:S(2)}) collective-permute-start(f32[5,4,4,16]{3,2,1,0:T(4,128)S(1)} %pad_maximum_fusion.11), channel_id=1, source_target_pairs={{0,4},{4,8},{8,12},{12,16},{16,20},{20,24},{24,28},{28,32},{32,36}... | collective-permute-start | bytes 15368 | tf_op jit(solution)/shard_map/ppermute | solution.py:30
  317.4 12.1 %collective-permute-start.17 = (f32[5,4,12,16]{3,2,1,0:T(8,128)S(1)}, f32[5,4,12,16]{3,2,1,0:T(8,128)S(1)}, u32[]{:S(2)}, u32[]{:S(2)}) collective-permute-start(f32[5,4,12,16]{3,2,1,0:T(8,128)S(1)} %pad_maximum_fusion.5), channel_id=1, source_target_pairs={{1,0},{2,1},{3,2},{0,3},{5,4},{6,5},{7,6},{4,7},{9,8},{10,9},{11,1... | collective-permute-start | bytes 46088 | tf_op jit(solution)/shard_map/ppermute | solution.py:32
  321.4 12.1 %collective-permute-start.16 = (f32[5,4,12,16]{3,2,1,0:T(8,128)S(1)}, f32[5,4,12,16]{3,2,1,0:T(8,128)S(1)}, u32[]{:S(2)}, u32[]{:S(2)}) collective-permute-start(f32[5,4,12,16]{3,2,1,0:T(8,128)S(1)} %pad_maximum_fusion.5), channel_id=1, source_target_pairs={{0,1},{1,2},{2,3},{3,0},{4,5},{5,6},{6,7},{7,4},{8,9},{9,10},{10,1... | collective-permute-start | bytes 46088 | tf_op jit(solution)/shard_map/ppermute | solution.py:30

commit v2 on v1

--- a/solution.py
+++ b/solution.py
@@ -38,6 +38,17 @@
 
 def by_axis(shard, axes):
     return functools.reduce(lax.psum, axes, shard)
+
+
+def group_sum(values, axes):
+    count = lax.axis_size(axes)
+    here = lax.axis_index(axes)
+    received = [values] + [
+        lax.ppermute(values, axes, [(j, (j - shift) % count) for j in range(count)])
+        for shift in range(1, count)
+    ]
+    ordered = jnp.roll(jnp.stack(received), here, axis=0)
+    return jnp.sum(ordered, axis=0)
 
 
 def column_gather(table, index):
@@ -253,7 +264,7 @@
             jnp.reshape(live_count.astype(jnp.float32), (1,)),
         ]
     )
-    summed = lax.psum(packed, GX_GY_GZ)
+    summed = functools.reduce(group_sum, (GX, GY, "gz"), packed)
     totals = summed[:10] / summed[10]
     return (forces, new_velocity, electron, totals)
 

time: 340 us -> 342 us (level); the launches traced: 339 us -> 337 us
  blocking collectives: 99.4 us -> 0 us
  starting transfers between devices: 61.1 us -> 153 us
  waiting for transfers between devices: 40.4 us -> 44.2 us
    psum x1 -> x0, blocking collectives: 99.4 us -> none  [local(): summed = lax.psum(packed, GX_GY_GZ)]
    ppermute x0 -> x25, starting transfers between devices: none -> 90 us  [group_sum(): lax.ppermute(values, axes, [(j, (j - shift) % count) for j in range(count)])]
    ppermute x0 -> x25, waiting for transfers between devices: none -> 6.89 us  [group_sum(): lax.ppermute(values, axes, [(j, (j - shift) % count) for j in range(count)])]
  transfers between devices with their start and end apart: 18 -> 43, of which waited for: 11 -> 14; matrix products, arithmetic and copies ran while one was open for 4% -> 5% of each run, Pallas kernels for 0% -> 0%
where the time goes in v2:
time: 342 us; the launch traced here: 337 us
  starting transfers between devices  153 us (45%)
  local copies, waits for them, and re-layouts  79 us (23%)
  waiting for transfers between devices  44.2 us (13%)
  other arithmetic  34.7 us (10%)
  matrix products  24.1 us (7%)
    ppermute x25, starting transfers between devices, group_sum(): lax.ppermute(values, axes, [(j, (j - shift) % count) for j in range(count)])  90 us
    ppermute x9, starting transfers between devices, padded(): lax.ppermute(head, axis, [((i + 1) % count, i) for i in range(count)])  48.7 us
    gather x2, local copies, waits for them, and re-layouts, local(): adjoint_table[:, neighbour_index]  48.4 us
    ppermute x9, waiting for transfers between devices, padded(): lax.ppermute(head, axis, [((i + 1) % count, i) for i in range(count)])  23.1 us
    ppermute x9, waiting for transfers between devices, padded(): lax.ppermute(tail, axis, [(i, (i + 1) % count) for i in range(count)])  14.3 us
    ppermute x9, starting transfers between devices, padded(): lax.ppermute(tail, axis, [(i, (i + 1) % count) for i in range(count)])  13.9 us
    dot_general x1, matrix products, atom_basis(): jnp.einsum('nka,mka->nma', shaped, harmonics(separation), precision=lax.P...  12.2 us
    ppermute x25, waiting for transfers between devices, group_sum(): lax.ppermute(values, axes, [(j, (j - shift) % count) for j in range(count)])  6.89 us
  transfers between devices with their start and end apart: 43, of which 14 were waited for; matrix products, arithmetic and copies ran while one was open for 5% of the time, Pallas kernels for 0%

profile of v2, /device:TPU:1, one launch (start us, length us, event | category | flops | bytes accessed | tf_op | source)
XLA Modules:
  0.0 337.2 jit_solution(1520281847220274112)
XLA Ops:
  4.3 7.0 %collective-permute-start.1 = (f32[1,1,1,3,128]{3,4,2,1,0:T(8,128)S(1)}, f32[1,1,1,3,128]{3,4,2,1,0:T(8,128)S(1)}, u32[]{:S(2)}, u32[]{:S(2)}) collective-permute-start(f32[1,1,1,3,128]{3,4,2,1,0:T(8,128)S(1)} %bitcast_select_fusion.1), channel_id=1, source_target_pairs={{64,0},{128,64},{192,128},{256,192},{320,256},{384,320},{448,384},... | collective-permute-start | bytes 4616 | tf_op jit(solution)/shard_map/ppermute | solution.py:32
  19.6 3.8 %collective-permute-start.3 = (f32[3,1,1,3,128]{4,2,3,1,0:T(1,128)S(1)}, f32[3,1,1,3,128]{4,2,3,1,0:T(1,128)S(1)}, u32[]{:S(2)}, u32[]{:S(2)}) collective-permute-start(f32[3,1,1,3,128]{4,2,3,1,0:T(1,128)S(1)} %pad_maximum_fusion.13), channel_id=1, source_target_pairs={{4,0},{8,4},{12,8},{16,12},{20,16},{24,20},{28,24},{32,28},{36,32}... | collective-permute-start | bytes 13832 | tf_op jit(solution)/shard_map/ppermute | solution.py:32
  24.6 9.1 %collective-permute-start.5 = (f32[3,3,1,3,128]{4,2,3,1,0:T(1,128)S(1)}, f32[3,3,1,3,128]{4,2,3,1,0:T(1,128)S(1)}, u32[]{:S(2)}, u32[]{:S(2)}) collective-permute-start(f32[3,3,1,3,128]{4,2,3,1,0:T(1,128)S(1)} %pad_maximum_fusion.12), channel_id=1, source_target_pairs={{1,0},{2,1},{3,2},{0,3},{5,4},{6,5},{7,6},{4,7},{9,8},{10,9},{11,1... | collective-permute-start | bytes 41480 | tf_op jit(solution)/shard_map/ppermute | solution.py:32
  35.7 4.5 %collective-permute-done.4 = f32[3,3,1,3,128]{4,2,3,1,0:T(1,128)S(1)} collective-permute-done((f32[3,3,1,3,128]{4,2,3,1,0:T(1,128)S(1)}, f32[3,3,1,3,128]{4,2,3,1,0:T(1,128)S(1)}, u32[]{:S(2)}, u32[]{:S(2)}) %collective-permute-start.4) | collective-permute-done | bytes 13856 | tf_op jit(solution)/shard_map/ppermute | solution.py:30
  41.1 3.3 fusion.7
  47.6 3.8 %copy.133 = f32[16,24,512]{1,0,2:T(8,128)} copy(f32[16,24,512]{2,0,1:T(8,128)S(1)} %fusion.10) | data formatting | bytes 1572864 | tf_op jit(solution)/shard_map/mul | solution.py:116
  51.4 3.7 %copy.132 = f32[16,24,512]{1,0,2:T(8,128)} copy(f32[16,24,512]{2,1,0:T(8,128)S(1)} %constant_dynamic-update-slice_fusion) | data formatting | bytes 1572864 | tf_op jit(solution)/shard_map/stack | solution.py:94
  55.1 12.2 %fusion.275 = f32[512,16,16]{2,1,0:T(8,128)} fusion(f32[16,24,512]{1,0,2:T(8,128)} %copy.132, f32[16,24,512]{1,0,2:T(8,128)} %copy.133), kind=kOutput, calls=%fused_computation.584 | convolution fusion | flops 37748736 | bytes 2097152 | tf_op jit(solution)/shard_map/nka,mka->nma/dot_general | solution.py:118
  67.4 2.8 copy.134
  71.4 3.7 %copy.135 = f32[16,512,16]{2,0,1:T(8,128)} copy(f32[16,512,16]{1,2,0:T(8,128)S(1)} %fusion.20) | data formatting | bytes 1048576 | tf_op jit(solution)/shard_map/mnp,pma->nma/dot_general | solution.py:131
  75.1 3.7 %copy.138 = f32[16,512,16]{2,0,1:T(8,128)} copy(f32[16,512,16]{1,2,0:T(8,128)S(1)} %fusion.19) | data formatting | bytes 1048576 | tf_op jit(solution)/shard_map/mpn,pma->nma/dot_general | solution.py:132
  78.8 6.2 %fusion.3 = (f32[512]{0:T(512)S(1)}, f32[16,16,512]{0,1,2:T(8,128)S(1)}) fusion(f32[16,512,16]{2,0,1:T(8,128)} %copy.135, f32[512,16,16]{2,1,0:T(8,128)} %fusion.275, f32[16,16]{0,1:T(8,128)S(1)} %broadcast_multiply_fusion.3, f32[16,512,16]{2,0,1:T(8,128)} %copy.138), kind=kLoop, calls=%fused_computation.16 | loop fusion | flops 523776 | bytes 2100224 | tf_op jit(solution)/shard_map/reduce_sum | solution.py:133
  85.0 5.0 %fusion.11 = f32[8,16,512]{2,0,1:T(8,128)S(1)} fusion(f32[16,16,512]{0,1,2:T(8,128)S(1)} %get-tuple-element.30, f32[16,8]{0,1:T(8,128)S(1)} %copy-done), kind=kOutput, calls=%fused_computation.26 | convolution fusion | flops 12582912 | bytes 786944 | tf_op jit(solution)/shard_map/nc,nma->cma/dot_general | solution.py:206
  91.1 5.6 %collective-permute-start.7 = (f32[1,1,1,128,128]{3,4,2,1,0:T(8,128)S(1)}, f32[1,1,1,128,128]{3,4,2,1,0:T(8,128)S(1)}, u32[]{:S(2)}, u32[]{:S(2)}) collective-permute-start(f32[1,1,1,128,128]{3,4,2,1,0:T(8,128)S(1)} %bitcast_select_fusion), channel_id=1, source_target_pairs={{64,0},{128,64},{192,128},{256,192},{320,256},{384,320},{448,384},... | collective-permute-start | bytes 196616 | tf_op jit(solution)/shard_map/ppermute | solution.py:32
  98.7 5.2 %collective-permute-done.6 = f32[1,1,1,128,128]{3,4,2,1,0:T(8,128)S(1)} collective-permute-done((f32[1,1,1,128,128]{3,4,2,1,0:T(8,128)S(1)}, f32[1,1,1,128,128]{3,4,2,1,0:T(8,128)S(1)}, u32[]{:S(2)}, u32[]{:S(2)}) %collective-permute-start.6) | collective-permute-done | bytes 65568 | tf_op jit(solution)/shard_map/ppermute | solution.py:30
  103.8 6.5 %collective-permute-start.9 = (f32[3,1,1,128,128]{3,4,2,1,0:T(8,128)S(1)}, f32[3,1,1,128,128]{3,4,2,1,0:T(8,128)S(1)}, u32[]{:S(2)}, u32[]{:S(2)}) collective-permute-start(f32[3,1,1,128,128]{3,4,2,1,0:T(8,128)S(1)} %pad_maximum_fusion.4), channel_id=1, source_target_pairs={{4,0},{8,4},{12,8},{16,12},{20,16},{24,20},{28,24},{32,28},{36,32}... | collective-permute-start | bytes 589832 | tf_op jit(solution)/shard_map/ppermute | solution.py:32
  115.7 4.3 %collective-permute-start.10 = (f32[3,3,1,128,128]{3,4,2,1,0:T(8,128)}, f32[3,3,1,128,128]{3,4,2,1,0:T(8,128)S(1)}, u32[]{:S(2)}, u32[]{:S(2)}) collective-permute-start(f32[3,3,1,128,128]{3,4,2,1,0:T(8,128)} %pad_maximum_fusion.2), channel_id=1, source_target_pairs={{0,1},{1,2},{2,3},{3,0},{4,5},{5,6},{6,7},{7,4},{8,9},{9,10},{10,1... | collective-permute-start | bytes 1769480 | tf_op jit(solution)/shard_map/ppermute | solution.py:30
  120.0 4.1 %scatter_custom_fusion.1 = f32[128]{0:T(128)S(1)} fusion(s32[512]{0:T(512)S(1)} %copy-done.9, f32[512]{0:T(512)S(1)} %fusion.251, f32[]{:T(128)} %constant.218.clone.1), kind=kCustom, calls=%fused_computation.573 | custom fusion | flops 512 | bytes 516 | tf_op jit(solution)/shard_map/scatter-add | solution.py:226
  126.8 17.3 %collective-permute-done.11 = f32[3,3,1,128,128]{3,4,2,1,0:T(8,128)S(1)} collective-permute-done((f32[3,3,1,128,128]{3,4,2,1,0:T(8,128)}, f32[3,3,1,128,128]{3,4,2,1,0:T(8,128)S(1)}, u32[]{:S(2)}, u32[]{:S(2)}) %collective-permute-start.11) | collective-permute-done | bytes 589856 | tf_op jit(solution)/shard_map/ppermute | solution.py:32
  145.1 41.6 %gather_fusion.2 = f32[12288,128]{1,0:T(8,128)} fusion(f32[128,3968]{0,1:T(8,128)S(1)} %pad_maximum_fusion, s32[12288]{0:T(1024)S(1)} %broadcast_clamp_fusion), kind=kCustom, calls=%fused_computation.2 | custom fusion | bytes 12632064 | tf_op jit(solution)/shard_map/gather | solution.py:214
  186.7 6.8 %copy.144 = f32[24,512,128]{1,0,2:T(8,128)} copy(f32[24,512,128]{2,1,0:T(8,128)} %bitcast.310) | data formatting | bytes 12582912 | tf_op jit(solution)/shard_map/gather | solution.py:214
  193.5 4.1 %multiply_reduce_fusion.3 = (f32[16,24,512]{2,1,0:T(8,128)S(1)}, f32[16,24,512]{2,1,0:T(8,128)S(1)}, f32[8,24,512]{2,1,0:T(8,128)S(1)}) fusion(f32[8,24,512]{2,1,0:T(8,128)S(1)} %broadcast_multiply_fusion.2, f32[8,16,512]{2,1,0:T(8,128)S(1)} %copy.140, f32[8,16,24,512]{3,2,1,0:T(8,128)} %bitcast.306, f32[16,24,512]{2,1,0:T(8,128)S(1)} %copy-done.2), kind=kLoop, calls=%fused_computation.10 | loop fusion | flops 8945664 | bytes 9699328 | tf_op jit(solution)/shard_map/jvp()/reduce_sum | solution.py:109
  201.1 4.1 %scatter_custom_fusion = f32[128]{0:T(128)S(1)} fusion(s32[512]{0:T(512)S(1)} %copy-done.9, f32[512]{0:T(512)S(1)} %fusion.252, f32[]{:T(128)} %constant.218.clone.1), kind=kCustom, calls=%fused_computation.575 | custom fusion | flops 512 | bytes 516 | tf_op jit(solution)/shard_map/scatter-add | solution.py:223
  207.5 5.5 %collective-permute-start.13 = (f32[5,4,4,4]{3,2,1,0:T(4,128)S(1)}, f32[5,4,4,4]{3,2,1,0:T(4,128)S(1)}, u32[]{:S(2)}, u32[]{:S(2)}) collective-permute-start(f32[5,4,4,4]{3,2,1,0:T(4,128)S(1)} %get-tuple-element.52), channel_id=1, source_target_pairs={{64,0},{128,64},{192,128},{256,192},{320,256},{384,320},{448,384},... | collective-permute-start | bytes 3848 | tf_op jit(solution)/shard_map/ppermute | solution.py:32
  214.1 3.7 %collective-permute-start.15 = (f32[5,4,4,16]{3,2,1,0:T(4,128)S(1)}, f32[5,4,4,16]{3,2,1,0:T(4,128)S(1)}, u32[]{:S(2)}, u32[]{:S(2)}) collective-permute-start(f32[5,4,4,16]{3,2,1,0:T(4,128)S(1)} %pad_maximum_fusion.11), channel_id=1, source_target_pairs={{4,0},{8,4},{12,8},{16,12},{20,16},{24,20},{28,24},{32,28},{36,32}... | collective-permute-start | bytes 15368 | tf_op jit(solution)/shard_map/ppermute | solution.py:32
  220.5 2.9 collective-permute-start.22
  223.5 5.3 %collective-permute-start.21 = (f32[11]{0:T(128)S(1)}, f32[11]{0:T(128)S(1)}, u32[]{:S(2)}, u32[]{:S(2)}) collective-permute-start(f32[11]{0:T(128)S(1)} %pad_maximum_fusion.14), channel_id=1, source_target_pairs={{0,256},{64,320},{128,384},{192,448},{256,0},{320,64},{384,128},{4... | collective-permute-start | bytes 140 | tf_op jit(solution)/shard_map/ppermute | solution.py:47
  231.1 4.9 %collective-permute-start.19 = (f32[11]{0:T(128)S(1)}, f32[11]{0:T(128)S(1)}, u32[]{:S(2)}, u32[]{:S(2)}) collective-permute-start(f32[11]{0:T(128)S(1)} %pad_maximum_fusion.14), channel_id=1, source_target_pairs={{0,384},{64,448},{128,0},{192,64},{256,128},{320,192},{384,256},{4... | collective-permute-start | bytes 140 | tf_op jit(solution)/shard_map/ppermute | solution.py:47
  235.9 3.7 %collective-permute-start.18 = (f32[11]{0:T(128)S(1)}, f32[11]{0:T(128)S(1)}, u32[]{:S(2)}, u32[]{:S(2)}) collective-permute-start(f32[11]{0:T(128)S(1)} %pad_maximum_fusion.14), channel_id=1, source_target_pairs={{0,448},{64,0},{128,64},{192,128},{256,192},{320,256},{384,320},{4... | collective-permute-start | bytes 140 | tf_op jit(solution)/shard_map/ppermute | solution.py:47
  241.6 4.5 %collective-permute-done.24 = f32[11]{0:T(128)S(1)} collective-permute-done((f32[11]{0:T(128)S(1)}, f32[11]{0:T(128)S(1)}, u32[]{:S(2)}, u32[]{:S(2)}) %collective-permute-start.24) | collective-permute-done | bytes 76 | tf_op jit(solution)/shard_map/ppermute | solution.py:47
  246.2 2.8 collective-permute-start.39
  248.9 3.3 collective-permute-start.38
  252.2 3.6 %collective-permute-start.37 = (f32[11]{0:T(128)S(1)}, f32[11]{0:T(128)S(1)}, u32[]{:S(2)}, u32[]{:S(2)}) collective-permute-start(f32[11]{0:T(128)S(1)} %dynamic-slice_reduce_fusion.1), channel_id=1, source_target_pairs={{0,12},{4,16},{8,20},{12,24},{16,28},{20,32},{24,36},{28,40},{32,4... | collective-permute-start | bytes 140 | tf_op jit(solution)/shard_map/ppermute | solution.py:47
  255.8 4.1 %collective-permute-start.36 = (f32[11]{0:T(128)S(1)}, f32[11]{0:T(128)S(1)}, u32[]{:S(2)}, u32[]{:S(2)}) collective-permute-start(f32[11]{0:T(128)S(1)} %dynamic-slice_reduce_fusion.1), channel_id=1, source_target_pairs={{0,16},{4,20},{8,24},{12,28},{16,32},{20,36},{24,40},{28,44},{32,4... | collective-permute-start | bytes 140 | tf_op jit(solution)/shard_map/ppermute | solution.py:47
  259.9 4.2 %collective-permute-start.35 = (f32[11]{0:T(128)S(1)}, f32[11]{0:T(128)S(1)}, u32[]{:S(2)}, u32[]{:S(2)}) collective-permute-start(f32[11]{0:T(128)S(1)} %dynamic-slice_reduce_fusion.1), channel_id=1, source_target_pairs={{0,20},{4,24},{8,28},{12,32},{16,36},{20,40},{24,44},{28,48},{32,5... | collective-permute-start | bytes 140 | tf_op jit(solution)/shard_map/ppermute | solution.py:47
  264.1 3.6 %collective-permute-start.34 = (f32[11]{0:T(128)S(1)}, f32[11]{0:T(128)S(1)}, u32[]{:S(2)}, u32[]{:S(2)}) collective-permute-start(f32[11]{0:T(128)S(1)} %dynamic-slice_reduce_fusion.1), channel_id=1, source_target_pairs={{0,24},{4,28},{8,32},{12,36},{16,40},{20,44},{24,48},{28,52},{32,5... | collective-permute-start | bytes 140 | tf_op jit(solution)/shard_map/ppermute | solution.py:47
  267.7 4.5 %collective-permute-start.33 = (f32[11]{0:T(128)S(1)}, f32[11]{0:T(128)S(1)}, u32[]{:S(2)}, u32[]{:S(2)}) collective-permute-start(f32[11]{0:T(128)S(1)} %dynamic-slice_reduce_fusion.1), channel_id=1, source_target_pairs={{0,28},{4,32},{8,36},{12,40},{16,44},{20,48},{24,52},{28,56},{32,6... | collective-permute-start | bytes 140 | tf_op jit(solution)/shard_map/ppermute | solution.py:47
  272.2 3.5 %collective-permute-start.32 = (f32[11]{0:T(128)S(1)}, f32[11]{0:T(128)S(1)}, u32[]{:S(2)}, u32[]{:S(2)}) collective-permute-start(f32[11]{0:T(128)S(1)} %dynamic-slice_reduce_fusion.1), channel_id=1, source_target_pairs={{0,32},{4,36},{8,40},{12,44},{16,48},{20,52},{24,56},{28,60},{32,0... | collective-permute-start | bytes 140 | tf_op jit(solution)/shard_map/ppermute | solution.py:47
  275.7 5.9 %collective-permute-start.31 = (f32[11]{0:T(128)S(1)}, f32[11]{0:T(128)S(1)}, u32[]{:S(2)}, u32[]{:S(2)}) collective-permute-start(f32[11]{0:T(128)S(1)} %dynamic-slice_reduce_fusion.1), channel_id=1, source_target_pairs={{0,36},{4,40},{8,44},{12,48},{16,52},{20,56},{24,60},{28,0},{32,4}... | collective-permute-start | bytes 140 | tf_op jit(solution)/shard_map/ppermute | solution.py:47
  281.6 5.6 %collective-permute-start.30 = (f32[11]{0:T(128)S(1)}, f32[11]{0:T(128)S(1)}, u32[]{:S(2)}, u32[]{:S(2)}) collective-permute-start(f32[11]{0:T(128)S(1)} %dynamic-slice_reduce_fusion.1), channel_id=1, source_target_pairs={{0,40},{4,44},{8,48},{12,52},{16,56},{20,60},{24,0},{28,4},{32,8},... | collective-permute-start | bytes 140 | tf_op jit(solution)/shard_map/ppermute | solution.py:47
  289.4 3.6 %collective-permute-start.28 = (f32[11]{0:T(128)S(1)}, f32[11]{0:T(128)S(1)}, u32[]{:S(2)}, u32[]{:S(2)}) collective-permute-start(f32[11]{0:T(128)S(1)} %dynamic-slice_reduce_fusion.1), channel_id=1, source_target_pairs={{0,48},{4,52},{8,56},{12,60},{16,0},{20,4},{24,8},{28,12},{32,16},... | collective-permute-start | bytes 140 | tf_op jit(solution)/shard_map/ppermute | solution.py:47
  295.7 4.6 %collective-permute-start.26 = (f32[11]{0:T(128)S(1)}, f32[11]{0:T(128)S(1)}, u32[]{:S(2)}, u32[]{:S(2)}) collective-permute-start(f32[11]{0:T(128)S(1)} %dynamic-slice_reduce_fusion.1), channel_id=1, source_target_pairs={{0,56},{4,60},{8,0},{12,4},{16,8},{20,12},{24,16},{28,20},{32,24},... | collective-permute-start | bytes 140 | tf_op jit(solution)/shard_map/ppermute | solution.py:47
  303.4 3.4 %collective-permute-start.42 = (f32[11]{0:T(128)S(1)}, f32[11]{0:T(128)S(1)}, u32[]{:S(2)}, u32[]{:S(2)}) collective-permute-start(f32[11]{0:T(128)S(1)} %dynamic-slice_reduce_fusion), channel_id=1, source_target_pairs={{0,1},{1,2},{2,3},{3,0},{4,5},{5,6},{6,7},{7,4},{8,9},{9,10},{10,1... | collective-permute-start | bytes 140 | tf_op jit(solution)/shard_map/ppermute | solution.py:47
  306.8 3.0 collective-permute-start.41
  309.8 5.5 %collective-permute-start.40 = (f32[11]{0:T(128)S(1)}, f32[11]{0:T(128)S(1)}, u32[]{:S(2)}, u32[]{:S(2)}) collective-permute-start(f32[11]{0:T(128)S(1)} %dynamic-slice_reduce_fusion), channel_id=1, source_target_pairs={{0,3},{1,0},{2,1},{3,2},{4,7},{5,4},{6,5},{7,6},{8,11},{9,8},{10,9... | collective-permute-start | bytes 140 | tf_op jit(solution)/shard_map/ppermute | solution.py:47
  316.8 5.7 %collective-permute-start.17 = (f32[5,4,12,16]{3,2,1,0:T(8,128)S(1)}, f32[5,4,12,16]{3,2,1,0:T(8,128)S(1)}, u32[]{:S(2)}, u32[]{:S(2)}) collective-permute-start(f32[5,4,12,16]{3,2,1,0:T(8,128)S(1)} %pad_maximum_fusion.5), channel_id=1, source_target_pairs={{1,0},{2,1},{3,2},{0,3},{5,4},{6,5},{7,6},{4,7},{9,8},{10,9},{11,1... | collective-permute-start | bytes 46088 | tf_op jit(solution)/shard_map/ppermute | solution.py:32
  325.6 3.6 %collective-permute-done.17 = f32[5,4,12,16]{3,2,1,0:T(8,128)S(1)} collective-permute-done((f32[5,4,12,16]{3,2,1,0:T(8,128)S(1)}, f32[5,4,12,16]{3,2,1,0:T(8,128)S(1)}, u32[]{:S(2)}, u32[]{:S(2)}) %collective-permute-start.17) | collective-permute-done | bytes 15392 | tf_op jit(solution)/shard_map/ppermute | solution.py:32
  333.2 3.3 gather_fusion.3
  (220 shorter events, 62.2 us)
Async XLA Ops:
  0.6 46.0 %copy-start = (f32[16,8]{0,1:T(8,128)S(1)}, f32[16,8]{0,1:T(8,128)}, u32[]{:S(2)}) copy-start(f32[16,8]{0,1:T(8,128)} %param.20) | copy-start | bytes 1540
  0.6 43.8 %copy-start.6 = (f32[3,512]{1,0:T(4,128)S(1)}, f32[3,512]{1,0:T(4,128)}, u32[]{:S(2)}) copy-start(f32[3,512]{1,0:T(4,128)} %param.13) | copy-start | bytes 18436
  4.3 15.2 %collective-permute-start.1 = (f32[1,1,1,3,128]{3,4,2,1,0:T(8,128)S(1)}, f32[1,1,1,3,128]{3,4,2,1,0:T(8,128)S(1)}, u32[]{:S(2)}, u32[]{:S(2)}) collective-permute-start(f32[1,1,1,3,128]{3,4,2,1,0:T(8,128)S(1)} %bitcast_select_fusion.1), channel_id=1, source_target_pairs={{64,0},{128,64},{192,128},{256,192},{320,256},{384,320},{448,384},... | collective-permute-start | bytes 4616 | tf_op jit(solution)/shard_map/ppermute | solution.py:32
  11.3 8.2 %collective-permute-start = (f32[1,1,1,3,128]{3,4,2,1,0:T(8,128)S(1)}, f32[1,1,1,3,128]{3,4,2,1,0:T(8,128)S(1)}, u32[]{:S(2)}, u32[]{:S(2)}) collective-permute-start(f32[1,1,1,3,128]{3,4,2,1,0:T(8,128)S(1)} %bitcast_select_fusion.1), channel_id=1, source_target_pairs={{0,64},{64,128},{128,192},{192,256},{256,320},{320,384},{384,448},... | collective-permute-start | bytes 4616 | tf_op jit(solution)/shard_map/ppermute | solution.py:30
  19.6 4.6 %collective-permute-start.3 = (f32[3,1,1,3,128]{4,2,3,1,0:T(1,128)S(1)}, f32[3,1,1,3,128]{4,2,3,1,0:T(1,128)S(1)}, u32[]{:S(2)}, u32[]{:S(2)}) collective-permute-start(f32[3,1,1,3,128]{4,2,3,1,0:T(1,128)S(1)} %pad_maximum_fusion.13), channel_id=1, source_target_pairs={{4,0},{8,4},{12,8},{16,12},{20,16},{24,20},{28,24},{32,28},{36,32}... | collective-permute-start | bytes 13832 | tf_op jit(solution)/shard_map/ppermute | solution.py:32
  23.4 1.2 collective-permute-start.2
  24.6 11.1 %collective-permute-start.5 = (f32[3,3,1,3,128]{4,2,3,1,0:T(1,128)S(1)}, f32[3,3,1,3,128]{4,2,3,1,0:T(1,128)S(1)}, u32[]{:S(2)}, u32[]{:S(2)}) collective-permute-start(f32[3,3,1,3,128]{4,2,3,1,0:T(1,128)S(1)} %pad_maximum_fusion.12), channel_id=1, source_target_pairs={{1,0},{2,1},{3,2},{0,3},{5,4},{6,5},{7,6},{4,7},{9,8},{10,9},{11,1... | collective-permute-start | bytes 41480 | tf_op jit(solution)/shard_map/ppermute | solution.py:32
  33.7 6.6 %collective-permute-start.4 = (f32[3,3,1,3,128]{4,2,3,1,0:T(1,128)S(1)}, f32[3,3,1,3,128]{4,2,3,1,0:T(1,128)S(1)}, u32[]{:S(2)}, u32[]{:S(2)}) collective-permute-start(f32[3,3,1,3,128]{4,2,3,1,0:T(1,128)S(1)} %pad_maximum_fusion.12), channel_id=1, source_target_pairs={{0,1},{1,2},{2,3},{3,0},{4,5},{5,6},{6,7},{7,4},{8,9},{9,10},{10,1... | collective-permute-start | bytes 41480 | tf_op jit(solution)/shard_map/ppermute | solution.py:30
  85.0 39.1 %copy-start.11 = (f32[4,4,8]{2,1,0:T(4,128)S(1)}, f32[4,4,8]{2,1,0:T(4,128)}, u32[]{:S(2)}) copy-start(f32[4,4,8]{2,1,0:T(4,128)} %param.25) | copy-start | bytes 1540
  85.0 40.8 %copy-start.12 = (f32[16]{0:T(128)S(1)}, f32[16]{0:T(128)}, u32[]{:S(2)}) copy-start(f32[16]{0:T(128)} %param.21) | copy-start | bytes 196
  91.1 7.6 %collective-permute-start.7 = (f32[1,1,1,128,128]{3,4,2,1,0:T(8,128)S(1)}, f32[1,1,1,128,128]{3,4,2,1,0:T(8,128)S(1)}, u32[]{:S(2)}, u32[]{:S(2)}) collective-permute-start(f32[1,1,1,128,128]{3,4,2,1,0:T(8,128)S(1)} %bitcast_select_fusion), channel_id=1, source_target_pairs={{64,0},{128,64},{192,128},{256,192},{320,256},{384,320},{448,384},... | collective-permute-start | bytes 196616 | tf_op jit(solution)/shard_map/ppermute | solution.py:32
  96.7 7.1 %collective-permute-start.6 = (f32[1,1,1,128,128]{3,4,2,1,0:T(8,128)S(1)}, f32[1,1,1,128,128]{3,4,2,1,0:T(8,128)S(1)}, u32[]{:S(2)}, u32[]{:S(2)}) collective-permute-start(f32[1,1,1,128,128]{3,4,2,1,0:T(8,128)S(1)} %bitcast_select_fusion), channel_id=1, source_target_pairs={{0,64},{64,128},{128,192},{192,256},{256,320},{320,384},{384,448},... | collective-permute-start | bytes 196616 | tf_op jit(solution)/shard_map/ppermute | solution.py:30
  103.8 7.5 %collective-permute-start.9 = (f32[3,1,1,128,128]{3,4,2,1,0:T(8,128)S(1)}, f32[3,1,1,128,128]{3,4,2,1,0:T(8,128)S(1)}, u32[]{:S(2)}, u32[]{:S(2)}) collective-permute-start(f32[3,1,1,128,128]{3,4,2,1,0:T(8,128)S(1)} %pad_maximum_fusion.4), channel_id=1, source_target_pairs={{4,0},{8,4},{12,8},{16,12},{20,16},{24,20},{28,24},{32,28},{36,32}... | collective-permute-start | bytes 589832 | tf_op jit(solution)/shard_map/ppermute | solution.py:32
  110.3 2.6 collective-permute-start.8
  113.8 30.3 %collective-permute-start.11 = (f32[3,3,1,128,128]{3,4,2,1,0:T(8,128)}, f32[3,3,1,128,128]{3,4,2,1,0:T(8,128)S(1)}, u32[]{:S(2)}, u32[]{:S(2)}) collective-permute-start(f32[3,3,1,128,128]{3,4,2,1,0:T(8,128)} %pad_maximum_fusion.2), channel_id=1, source_target_pairs={{1,0},{2,1},{3,2},{0,3},{5,4},{6,5},{7,6},{4,7},{9,8},{10,9},{11,1... | collective-permute-start | bytes 1769480 | tf_op jit(solution)/shard_map/ppermute | solution.py:32
  115.7 29.1 %collective-permute-start.10 = (f32[3,3,1,128,128]{3,4,2,1,0:T(8,128)}, f32[3,3,1,128,128]{3,4,2,1,0:T(8,128)S(1)}, u32[]{:S(2)}, u32[]{:S(2)}) collective-permute-start(f32[3,3,1,128,128]{3,4,2,1,0:T(8,128)} %pad_maximum_fusion.2), channel_id=1, source_target_pairs={{0,1},{1,2},{2,3},{3,0},{4,5},{5,6},{6,7},{7,4},{8,9},{9,10},{10,1... | collective-permute-start | bytes 1769480 | tf_op jit(solution)/shard_map/ppermute | solution.py:30
  199.9 136.7 %copy-start.7 = (f32[3,512]{1,0:T(4,128)}, f32[3,512]{1,0:T(4,128)S(1)}, u32[]{:S(2)}) copy-start(f32[3,512]{1,0:T(4,128)S(1)} %get-tuple-element.25) | copy-start | bytes 18436
  205.5 8.1 %collective-permute-start.12 = (f32[5,4,4,4]{3,2,1,0:T(4,128)S(1)}, f32[5,4,4,4]{3,2,1,0:T(4,128)S(1)}, u32[]{:S(2)}, u32[]{:S(2)}) collective-permute-start(f32[5,4,4,4]{3,2,1,0:T(4,128)S(1)} %get-tuple-element.51), channel_id=1, source_target_pairs={{0,64},{64,128},{128,192},{192,256},{256,320},{320,384},{384,448},... | collective-permute-start | bytes 3848 | tf_op jit(solution)/shard_map/ppermute | solution.py:30
  207.5 6.6 %collective-permute-start.13 = (f32[5,4,4,4]{3,2,1,0:T(4,128)S(1)}, f32[5,4,4,4]{3,2,1,0:T(4,128)S(1)}, u32[]{:S(2)}, u32[]{:S(2)}) collective-permute-start(f32[5,4,4,4]{3,2,1,0:T(4,128)S(1)} %get-tuple-element.52), channel_id=1, source_target_pairs={{64,0},{128,64},{192,128},{256,192},{320,256},{384,320},{448,384},... | collective-permute-start | bytes 3848 | tf_op jit(solution)/shard_map/ppermute | solution.py:32
  214.1 102.5 %collective-permute-start.15 = (f32[5,4,4,16]{3,2,1,0:T(4,128)S(1)}, f32[5,4,4,16]{3,2,1,0:T(4,128)S(1)}, u32[]{:S(2)}, u32[]{:S(2)}) collective-permute-start(f32[5,4,4,16]{3,2,1,0:T(4,128)S(1)} %pad_maximum_fusion.11), channel_id=1, source_target_pairs={{4,0},{8,4},{12,8},{16,12},{20,16},{24,20},{28,24},{32,28},{36,32}... | collective-permute-start | bytes 15368 | tf_op jit(solution)/shard_map/ppermute | solution.py:32
  217.8 98.9 %collective-permute-start.14 = (f32[5,4,4,16]{3,2,1,0:T(4,128)S(1)}, f32[5,4,4,16]{3,2,1,0:T(4,128)S(1)}, u32[]{:S(2)}, u32[]{:S(2)}) collective-permute-start(f32[5,4,4,16]{3,2,1,0:T(4,128)S(1)} %pad_maximum_fusion.11), channel_id=1, source_target_pairs={{0,4},{4,8},{8,12},{12,16},{16,20},{20,24},{24,28},{28,32},{32,36}... | collective-permute-start | bytes 15368 | tf_op jit(solution)/shard_map/ppermute | solution.py:30
  218.6 10.2 %collective-permute-start.23 = (f32[11]{0:T(128)S(1)}, f32[11]{0:T(128)S(1)}, u32[]{:S(2)}, u32[]{:S(2)}) collective-permute-start(f32[11]{0:T(128)S(1)} %pad_maximum_fusion.14), channel_id=1, source_target_pairs={{0,128},{64,192},{128,256},{192,320},{256,384},{320,448},{384,0},{... | collective-permute-start | bytes 140 | tf_op jit(solution)/shard_map/ppermute | solution.py:47
  220.5 10.5 %collective-permute-start.22 = (f32[11]{0:T(128)S(1)}, f32[11]{0:T(128)S(1)}, u32[]{:S(2)}, u32[]{:S(2)}) collective-permute-start(f32[11]{0:T(128)S(1)} %pad_maximum_fusion.14), channel_id=1, source_target_pairs={{0,192},{64,256},{128,320},{192,384},{256,448},{320,0},{384,64},{4... | collective-permute-start | bytes 140 | tf_op jit(solution)/shard_map/ppermute | solution.py:47
  223.5 12.5 %collective-permute-start.21 = (f32[11]{0:T(128)S(1)}, f32[11]{0:T(128)S(1)}, u32[]{:S(2)}, u32[]{:S(2)}) collective-permute-start(f32[11]{0:T(128)S(1)} %pad_maximum_fusion.14), channel_id=1, source_target_pairs={{0,256},{64,320},{128,384},{192,448},{256,0},{320,64},{384,128},{4... | collective-permute-start | bytes 140 | tf_op jit(solution)/shard_map/ppermute | solution.py:47
  228.8 10.8 %collective-permute-start.20 = (f32[11]{0:T(128)S(1)}, f32[11]{0:T(128)S(1)}, u32[]{:S(2)}, u32[]{:S(2)}) collective-permute-start(f32[11]{0:T(128)S(1)} %pad_maximum_fusion.14), channel_id=1, source_target_pairs={{0,320},{64,384},{128,448},{192,0},{256,64},{320,128},{384,192},{4... | collective-permute-start | bytes 140 | tf_op jit(solution)/shard_map/ppermute | solution.py:47
  231.1 10.5 %collective-permute-start.19 = (f32[11]{0:T(128)S(1)}, f32[11]{0:T(128)S(1)}, u32[]{:S(2)}, u32[]{:S(2)}) collective-permute-start(f32[11]{0:T(128)S(1)} %pad_maximum_fusion.14), channel_id=1, source_target_pairs={{0,384},{64,448},{128,0},{192,64},{256,128},{320,192},{384,256},{4... | collective-permute-start | bytes 140 | tf_op jit(solution)/shard_map/ppermute | solution.py:47
  235.9 5.7 %collective-permute-start.18 = (f32[11]{0:T(128)S(1)}, f32[11]{0:T(128)S(1)}, u32[]{:S(2)}, u32[]{:S(2)}) collective-permute-start(f32[11]{0:T(128)S(1)} %pad_maximum_fusion.14), channel_id=1, source_target_pairs={{0,448},{64,0},{128,64},{192,128},{256,192},{320,256},{384,320},{4... | collective-permute-start | bytes 140 | tf_op jit(solution)/shard_map/ppermute | solution.py:47
  239.7 6.4 %collective-permute-start.24 = (f32[11]{0:T(128)S(1)}, f32[11]{0:T(128)S(1)}, u32[]{:S(2)}, u32[]{:S(2)}) collective-permute-start(f32[11]{0:T(128)S(1)} %pad_maximum_fusion.14), channel_id=1, source_target_pairs={{0,64},{64,128},{128,192},{192,256},{256,320},{320,384},{384,448},... | collective-permute-start | bytes 140 | tf_op jit(solution)/shard_map/ppermute | solution.py:47
  246.2 9.7 %collective-permute-start.39 = (f32[11]{0:T(128)S(1)}, f32[11]{0:T(128)S(1)}, u32[]{:S(2)}, u32[]{:S(2)}) collective-permute-start(f32[11]{0:T(128)S(1)} %dynamic-slice_reduce_fusion.1), channel_id=1, source_target_pairs={{0,4},{4,8},{8,12},{12,16},{16,20},{20,24},{24,28},{28,32},{32,36}... | collective-permute-start | bytes 140 | tf_op jit(solution)/shard_map/ppermute | solution.py:47
  248.9 11.0 %collective-permute-start.38 = (f32[11]{0:T(128)S(1)}, f32[11]{0:T(128)S(1)}, u32[]{:S(2)}, u32[]{:S(2)}) collective-permute-start(f32[11]{0:T(128)S(1)} %dynamic-slice_reduce_fusion.1), channel_id=1, source_target_pairs={{0,8},{4,12},{8,16},{12,20},{16,24},{20,28},{24,32},{28,36},{32,40... | collective-permute-start | bytes 140 | tf_op jit(solution)/shard_map/ppermute | solution.py:47
  252.2 11.9 %collective-permute-start.37 = (f32[11]{0:T(128)S(1)}, f32[11]{0:T(128)S(1)}, u32[]{:S(2)}, u32[]{:S(2)}) collective-permute-start(f32[11]{0:T(128)S(1)} %dynamic-slice_reduce_fusion.1), channel_id=1, source_target_pairs={{0,12},{4,16},{8,20},{12,24},{16,28},{20,32},{24,36},{28,40},{32,4... | collective-permute-start | bytes 140 | tf_op jit(solution)/shard_map/ppermute | solution.py:47
  255.8 11.9 %collective-permute-start.36 = (f32[11]{0:T(128)S(1)}, f32[11]{0:T(128)S(1)}, u32[]{:S(2)}, u32[]{:S(2)}) collective-permute-start(f32[11]{0:T(128)S(1)} %dynamic-slice_reduce_fusion.1), channel_id=1, source_target_pairs={{0,16},{4,20},{8,24},{12,28},{16,32},{20,36},{24,40},{28,44},{32,4... | collective-permute-start | bytes 140 | tf_op jit(solution)/shard_map/ppermute | solution.py:47
  259.9 12.3 %collective-permute-start.35 = (f32[11]{0:T(128)S(1)}, f32[11]{0:T(128)S(1)}, u32[]{:S(2)}, u32[]{:S(2)}) collective-permute-start(f32[11]{0:T(128)S(1)} %dynamic-slice_reduce_fusion.1), channel_id=1, source_target_pairs={{0,20},{4,24},{8,28},{12,32},{16,36},{20,40},{24,44},{28,48},{32,5... | collective-permute-start | bytes 140 | tf_op jit(solution)/shard_map/ppermute | solution.py:47
  264.1 11.5 %collective-permute-start.34 = (f32[11]{0:T(128)S(1)}, f32[11]{0:T(128)S(1)}, u32[]{:S(2)}, u32[]{:S(2)}) collective-permute-start(f32[11]{0:T(128)S(1)} %dynamic-slice_reduce_fusion.1), channel_id=1, source_target_pairs={{0,24},{4,28},{8,32},{12,36},{16,40},{20,44},{24,48},{28,52},{32,5... | collective-permute-start | bytes 140 | tf_op jit(solution)/shard_map/ppermute | solution.py:47
  267.7 13.9 %collective-permute-start.33 = (f32[11]{0:T(128)S(1)}, f32[11]{0:T(128)S(1)}, u32[]{:S(2)}, u32[]{:S(2)}) collective-permute-start(f32[11]{0:T(128)S(1)} %dynamic-slice_reduce_fusion.1), channel_id=1, source_target_pairs={{0,28},{4,32},{8,36},{12,40},{16,44},{20,48},{24,52},{28,56},{32,6... | collective-permute-start | bytes 140 | tf_op jit(solution)/shard_map/ppermute | solution.py:47
  272.2 15.0 %collective-permute-start.32 = (f32[11]{0:T(128)S(1)}, f32[11]{0:T(128)S(1)}, u32[]{:S(2)}, u32[]{:S(2)}) collective-permute-start(f32[11]{0:T(128)S(1)} %dynamic-slice_reduce_fusion.1), channel_id=1, source_target_pairs={{0,32},{4,36},{8,40},{12,44},{16,48},{20,52},{24,56},{28,60},{32,0... | collective-permute-start | bytes 140 | tf_op jit(solution)/shard_map/ppermute | solution.py:47
  275.7 13.7 %collective-permute-start.31 = (f32[11]{0:T(128)S(1)}, f32[11]{0:T(128)S(1)}, u32[]{:S(2)}, u32[]{:S(2)}) collective-permute-start(f32[11]{0:T(128)S(1)} %dynamic-slice_reduce_fusion.1), channel_id=1, source_target_pairs={{0,36},{4,40},{8,44},{12,48},{16,52},{20,56},{24,60},{28,0},{32,4}... | collective-permute-start | bytes 140 | tf_op jit(solution)/shard_map/ppermute | solution.py:47
  281.6 11.5 %collective-permute-start.30 = (f32[11]{0:T(128)S(1)}, f32[11]{0:T(128)S(1)}, u32[]{:S(2)}, u32[]{:S(2)}) collective-permute-start(f32[11]{0:T(128)S(1)} %dynamic-slice_reduce_fusion.1), channel_id=1, source_target_pairs={{0,40},{4,44},{8,48},{12,52},{16,56},{20,60},{24,0},{28,4},{32,8},... | collective-permute-start | bytes 140 | tf_op jit(solution)/shard_map/ppermute | solution.py:47
  287.2 8.5 %collective-permute-start.29 = (f32[11]{0:T(128)S(1)}, f32[11]{0:T(128)S(1)}, u32[]{:S(2)}, u32[]{:S(2)}) collective-permute-start(f32[11]{0:T(128)S(1)} %dynamic-slice_reduce_fusion.1), channel_id=1, source_target_pairs={{0,44},{4,48},{8,52},{12,56},{16,60},{20,0},{24,4},{28,8},{32,12},... | collective-permute-start | bytes 140 | tf_op jit(solution)/shard_map/ppermute | solution.py:47
  289.4 10.8 %collective-permute-start.28 = (f32[11]{0:T(128)S(1)}, f32[11]{0:T(128)S(1)}, u32[]{:S(2)}, u32[]{:S(2)}) collective-permute-start(f32[11]{0:T(128)S(1)} %dynamic-slice_reduce_fusion.1), channel_id=1, source_target_pairs={{0,48},{4,52},{8,56},{12,60},{16,0},{20,4},{24,8},{28,12},{32,16},... | collective-permute-start | bytes 140 | tf_op jit(solution)/shard_map/ppermute | solution.py:47
  293.1 8.5 %collective-permute-start.27 = (f32[11]{0:T(128)S(1)}, f32[11]{0:T(128)S(1)}, u32[]{:S(2)}, u32[]{:S(2)}) collective-permute-start(f32[11]{0:T(128)S(1)} %dynamic-slice_reduce_fusion.1), channel_id=1, source_target_pairs={{0,52},{4,56},{8,60},{12,0},{16,4},{20,8},{24,12},{28,16},{32,20},... | collective-permute-start | bytes 140 | tf_op jit(solution)/shard_map/ppermute | solution.py:47
  295.7 5.9 %collective-permute-start.26 = (f32[11]{0:T(128)S(1)}, f32[11]{0:T(128)S(1)}, u32[]{:S(2)}, u32[]{:S(2)}) collective-permute-start(f32[11]{0:T(128)S(1)} %dynamic-slice_reduce_fusion.1), channel_id=1, source_target_pairs={{0,56},{4,60},{8,0},{12,4},{16,8},{20,12},{24,16},{28,20},{32,24},... | collective-permute-start | bytes 140 | tf_op jit(solution)/shard_map/ppermute | solution.py:47
  300.2 3.0 collective-permute-start.25
  303.4 12.0 %collective-permute-start.42 = (f32[11]{0:T(128)S(1)}, f32[11]{0:T(128)S(1)}, u32[]{:S(2)}, u32[]{:S(2)}) collective-permute-start(f32[11]{0:T(128)S(1)} %dynamic-slice_reduce_fusion), channel_id=1, source_target_pairs={{0,1},{1,2},{2,3},{3,0},{4,5},{5,6},{6,7},{7,4},{8,9},{9,10},{10,1... | collective-permute-start | bytes 140 | tf_op jit(solution)/shard_map/ppermute | solution.py:47
  306.8 8.5 %collective-permute-start.41 = (f32[11]{0:T(128)S(1)}, f32[11]{0:T(128)S(1)}, u32[]{:S(2)}, u32[]{:S(2)}) collective-permute-start(f32[11]{0:T(128)S(1)} %dynamic-slice_reduce_fusion), channel_id=1, source_target_pairs={{0,2},{1,3},{2,0},{3,1},{4,6},{5,7},{6,4},{7,5},{8,10},{9,11},{10,... | collective-permute-start | bytes 140 | tf_op jit(solution)/shard_map/ppermute | solution.py:47
  309.8 6.2 %collective-permute-start.40 = (f32[11]{0:T(128)S(1)}, f32[11]{0:T(128)S(1)}, u32[]{:S(2)}, u32[]{:S(2)}) collective-permute-start(f32[11]{0:T(128)S(1)} %dynamic-slice_reduce_fusion), channel_id=1, source_target_pairs={{0,3},{1,0},{2,1},{3,2},{4,7},{5,4},{6,5},{7,6},{8,11},{9,8},{10,9... | collective-permute-start | bytes 140 | tf_op jit(solution)/shard_map/ppermute | solution.py:47
  316.8 12.4 %collective-permute-start.17 = (f32[5,4,12,16]{3,2,1,0:T(8,128)S(1)}, f32[5,4,12,16]{3,2,1,0:T(8,128)S(1)}, u32[]{:S(2)}, u32[]{:S(2)}) collective-permute-start(f32[5,4,12,16]{3,2,1,0:T(8,128)S(1)} %pad_maximum_fusion.5), channel_id=1, source_target_pairs={{1,0},{2,1},{3,2},{0,3},{5,4},{6,5},{7,6},{4,7},{9,8},{10,9},{11,1... | collective-permute-start | bytes 46088 | tf_op jit(solution)/shard_map/ppermute | solution.py:32
  322.6 8.7 %collective-permute-start.16 = (f32[5,4,12,16]{3,2,1,0:T(8,128)S(1)}, f32[5,4,12,16]{3,2,1,0:T(8,128)S(1)}, u32[]{:S(2)}, u32[]{:S(2)}) collective-permute-start(f32[5,4,12,16]{3,2,1,0:T(8,128)S(1)} %pad_maximum_fusion.5), channel_id=1, source_target_pairs={{0,1},{1,2},{2,3},{3,0},{4,5},{5,6},{6,7},{7,4},{8,9},{9,10},{10,1... | collective-permute-start | bytes 46088 | tf_op jit(solution)/shard_map/ppermute | solution.py:30
  (10 other events, 95.7 us)

commit v3 on v2

--- a/solution.py
+++ b/solution.py
@@ -264,7 +264,7 @@
             jnp.reshape(live_count.astype(jnp.float32), (1,)),
         ]
     )
-    summed = functools.reduce(group_sum, (GX, GY, "gz"), packed)
+    summed = by_axis(packed, GX_GY_GZ)
     totals = summed[:10] / summed[10]
     return (forces, new_velocity, electron, totals)
 

time: 342 us -> 287 us (0.84); the launches traced: 337 us -> 286 us
  starting transfers between devices: 153 us -> 59.2 us
  blocking collectives: 0 us -> 44.2 us
    ppermute x25 -> x0, starting transfers between devices: 90 us -> none  [group_sum(): lax.ppermute(values, axes, [(j, (j - shift) % count) for j in range(count)])]
    psum x0 -> x5, blocking collectives: none -> 44.2 us  [by_axis(): return functools.reduce(lax.psum, axes, shard)]
    ppermute x9, starting transfers between devices: 48.7 us -> 41 us  [padded(): lax.ppermute(head, axis, [((i + 1) % count, i) for i in range(count)])]
    ppermute x25 -> x0, waiting for transfers between devices: 6.89 us -> none  [group_sum(): lax.ppermute(values, axes, [(j, (j - shift) % count) for j in range(count)])]
    ppermute x9, waiting for transfers between devices: 23.1 us -> 27.7 us  [padded(): lax.ppermute(head, axis, [((i + 1) % count, i) for i in range(count)])]
    ppermute x9, starting transfers between devices: 13.9 us -> 18.2 us  [padded(): lax.ppermute(tail, axis, [(i, (i + 1) % count) for i in range(count)])]
  transfers between devices with their start and end apart: 43 -> 18, of which waited for: 14 -> 10; matrix products, arithmetic and copies ran while one was open for 5% -> 4% of each run, Pallas kernels for 0% -> 0%
where the time goes in v3:
time: 287 us; the launch traced here: 286 us
  local copies, waits for them, and re-layouts  78.3 us (27%)
  starting transfers between devices  59.2 us (21%)
  waiting for transfers between devices  44.2 us (15%)
  blocking collectives  44.2 us (15%)
  other arithmetic  33.9 us (12%)
  matrix products  24 us (8%)
    gather x2, local copies, waits for them, and re-layouts, local(): adjoint_table[:, neighbour_index]  48 us
    psum x5, blocking collectives, by_axis(): return functools.reduce(lax.psum, axes, shard)  44.2 us
    ppermute x9, starting transfers between devices, padded(): lax.ppermute(head, axis, [((i + 1) % count, i) for i in range(count)])  41 us
    ppermute x9, waiting for transfers between devices, padded(): lax.ppermute(head, axis, [((i + 1) % count, i) for i in range(count)])  27.7 us
    ppermute x9, starting transfers between devices, padded(): lax.ppermute(tail, axis, [(i, (i + 1) % count) for i in range(count)])  18.2 us
    ppermute x9, waiting for transfers between devices, padded(): lax.ppermute(tail, axis, [(i, (i + 1) % count) for i in range(count)])  16.5 us
    dot_general x1, matrix products, atom_basis(): jnp.einsum('nka,mka->nma', shaped, harmonics(separation), precision=lax.P...  12.2 us
    reduce_sum x1, other arithmetic, adjoints(): jnp.sum(basis_sum * forward, axis=(0, 1))  6.22 us
  transfers between devices with their start and end apart: 18, of which 10 were waited for; matrix products, arithmetic and copies ran while one was open for 4% of the time, Pallas kernels for 0%

profile of v3, /device:TPU:1, one launch (start us, length us, event | category | flops | bytes accessed | tf_op | source)
XLA Modules:
  0.0 286.0 jit_solution(14538186477654669080)
XLA Ops:
  4.3 7.0 %collective-permute-start.1 = (f32[1,1,1,3,128]{3,4,2,1,0:T(8,128)S(1)}, f32[1,1,1,3,128]{3,4,2,1,0:T(8,128)S(1)}, u32[]{:S(2)}, u32[]{:S(2)}) collective-permute-start(f32[1,1,1,3,128]{3,4,2,1,0:T(8,128)S(1)} %bitcast_select_fusion.1), channel_id=1, source_target_pairs={{64,0},{128,64},{192,128},{256,192},{320,256},{384,320},{448,384},... | collective-permute-start | bytes 4616 | tf_op jit(solution)/shard_map/ppermute | solution.py:32
  11.3 1.9 collective-permute-start
  19.6 3.8 %collective-permute-start.3 = (f32[3,1,1,3,128]{4,2,3,1,0:T(1,128)S(1)}, f32[3,1,1,3,128]{4,2,3,1,0:T(1,128)S(1)}, u32[]{:S(2)}, u32[]{:S(2)}) collective-permute-start(f32[3,1,1,3,128]{4,2,3,1,0:T(1,128)S(1)} %pad_maximum_fusion.13), channel_id=1, source_target_pairs={{4,0},{8,4},{12,8},{16,12},{20,16},{24,20},{28,24},{32,28},{36,32}... | collective-permute-start | bytes 13832 | tf_op jit(solution)/shard_map/ppermute | solution.py:32
  24.5 9.1 %collective-permute-start.5 = (f32[3,3,1,3,128]{4,2,3,1,0:T(1,128)S(1)}, f32[3,3,1,3,128]{4,2,3,1,0:T(1,128)S(1)}, u32[]{:S(2)}, u32[]{:S(2)}) collective-permute-start(f32[3,3,1,3,128]{4,2,3,1,0:T(1,128)S(1)} %pad_maximum_fusion.12), channel_id=1, source_target_pairs={{1,0},{2,1},{3,2},{0,3},{5,4},{6,5},{7,6},{4,7},{9,8},{10,9},{11,1... | collective-permute-start | bytes 41480 | tf_op jit(solution)/shard_map/ppermute | solution.py:32
  33.6 1.9 collective-permute-start.4
  35.7 4.5 %collective-permute-done.4 = f32[3,3,1,3,128]{4,2,3,1,0:T(1,128)S(1)} collective-permute-done((f32[3,3,1,3,128]{4,2,3,1,0:T(1,128)S(1)}, f32[3,3,1,3,128]{4,2,3,1,0:T(1,128)S(1)}, u32[]{:S(2)}, u32[]{:S(2)}) %collective-permute-start.4) | collective-permute-done | bytes 13856 | tf_op jit(solution)/shard_map/ppermute | solution.py:30
  41.1 3.3 %fusion.7 = f32[3,12288]{1,0:T(4,128)S(1)} fusion(f32[3,31,128]{2,1,0:T(8,128)S(1)} %dot_general.28, s32[12288]{0:T(1024)S(1)} %get-tuple-element.50, pred[31,12288]{1,0:T(8,128)(4,1)S(1)} %iota_compare_fusion.1), kind=kOutput, calls=%fused_computation.22 | convolution fusion | flops 1759137792 | bytes 625152 | tf_op jit(solution)/shard_map/dot_general | solution.py:63
  46.6 1.0 fusion.10
  47.5 3.8 %copy.133 = f32[16,24,512]{1,0,2:T(8,128)} copy(f32[16,24,512]{2,0,1:T(8,128)S(1)} %fusion.10) | data formatting | bytes 1572864 | tf_op jit(solution)/shard_map/mul | solution.py:116
  51.3 3.7 %copy.132 = f32[16,24,512]{1,0,2:T(8,128)} copy(f32[16,24,512]{2,1,0:T(8,128)S(1)} %constant_dynamic-update-slice_fusion) | data formatting | bytes 1572864 | tf_op jit(solution)/shard_map/stack | solution.py:94
  55.0 12.2 %fusion.275 = f32[512,16,16]{2,1,0:T(8,128)} fusion(f32[16,24,512]{1,0,2:T(8,128)} %copy.132, f32[16,24,512]{1,0,2:T(8,128)} %copy.133), kind=kOutput, calls=%fused_computation.581 | convolution fusion | flops 37748736 | bytes 2097152 | tf_op jit(solution)/shard_map/nka,mka->nma/dot_general | solution.py:118
  67.2 2.8 copy.134
  71.2 3.7 %copy.135 = f32[16,512,16]{2,0,1:T(8,128)} copy(f32[16,512,16]{1,2,0:T(8,128)S(1)} %fusion.20) | data formatting | bytes 1048576 | tf_op jit(solution)/shard_map/mnp,pma->nma/dot_general | solution.py:131
  74.9 3.6 %copy.138 = f32[16,512,16]{2,0,1:T(8,128)} copy(f32[16,512,16]{1,2,0:T(8,128)S(1)} %fusion.19) | data formatting | bytes 1048576 | tf_op jit(solution)/shard_map/mpn,pma->nma/dot_general | solution.py:132
  78.5 6.2 %fusion.3 = (f32[512]{0:T(512)S(1)}, f32[16,16,512]{0,1,2:T(8,128)S(1)}) fusion(f32[16,512,16]{2,0,1:T(8,128)} %copy.135, f32[512,16,16]{2,1,0:T(8,128)} %fusion.275, f32[16,16]{0,1:T(8,128)S(1)} %broadcast_multiply_fusion.3, f32[16,512,16]{2,0,1:T(8,128)} %copy.138), kind=kLoop, calls=%fused_computation.16 | loop fusion | flops 523776 | bytes 2100224 | tf_op jit(solution)/shard_map/reduce_sum | solution.py:133
  84.8 5.0 %fusion.11 = f32[8,16,512]{2,0,1:T(8,128)S(1)} fusion(f32[16,16,512]{0,1,2:T(8,128)S(1)} %get-tuple-element.30, f32[16,8]{0,1:T(8,128)S(1)} %copy-done), kind=kOutput, calls=%fused_computation.26 | convolution fusion | flops 12582912 | bytes 786944 | tf_op jit(solution)/shard_map/nc,nma->cma/dot_general | solution.py:206
  90.8 5.6 %collective-permute-start.7 = (f32[1,1,1,128,128]{3,4,2,1,0:T(8,128)S(1)}, f32[1,1,1,128,128]{3,4,2,1,0:T(8,128)S(1)}, u32[]{:S(2)}, u32[]{:S(2)}) collective-permute-start(f32[1,1,1,128,128]{3,4,2,1,0:T(8,128)S(1)} %bitcast_select_fusion), channel_id=1, source_target_pairs={{64,0},{128,64},{192,128},{256,192},{320,256},{384,320},{448,384},... | collective-permute-start | bytes 196616 | tf_op jit(solution)/shard_map/ppermute | solution.py:32
  96.4 1.9 collective-permute-start.6
  98.4 5.2 %collective-permute-done.6 = f32[1,1,1,128,128]{3,4,2,1,0:T(8,128)S(1)} collective-permute-done((f32[1,1,1,128,128]{3,4,2,1,0:T(8,128)S(1)}, f32[1,1,1,128,128]{3,4,2,1,0:T(8,128)S(1)}, u32[]{:S(2)}, u32[]{:S(2)}) %collective-permute-start.6) | collective-permute-done | bytes 65568 | tf_op jit(solution)/shard_map/ppermute | solution.py:30
  103.6 6.5 %collective-permute-start.9 = (f32[3,1,1,128,128]{3,4,2,1,0:T(8,128)S(1)}, f32[3,1,1,128,128]{3,4,2,1,0:T(8,128)S(1)}, u32[]{:S(2)}, u32[]{:S(2)}) collective-permute-start(f32[3,1,1,128,128]{3,4,2,1,0:T(8,128)S(1)} %pad_maximum_fusion.4), channel_id=1, source_target_pairs={{4,0},{8,4},{12,8},{16,12},{20,16},{24,20},{28,24},{32,28},{36,32}... | collective-permute-start | bytes 589832 | tf_op jit(solution)/shard_map/ppermute | solution.py:32
  110.0 1.1 collective-permute-done.9
  111.1 1.5 collective-permute-done.8
  112.6 0.9 pad_maximum_fusion.2
  113.5 1.9 collective-permute-start.11
  115.4 4.3 %collective-permute-start.10 = (f32[3,3,1,128,128]{3,4,2,1,0:T(8,128)}, f32[3,3,1,128,128]{3,4,2,1,0:T(8,128)S(1)}, u32[]{:S(2)}, u32[]{:S(2)}) collective-permute-start(f32[3,3,1,128,128]{3,4,2,1,0:T(8,128)} %pad_maximum_fusion.2), channel_id=1, source_target_pairs={{0,1},{1,2},{2,3},{3,0},{4,5},{5,6},{6,7},{7,4},{8,9},{9,10},{10,1... | collective-permute-start | bytes 1769480 | tf_op jit(solution)/shard_map/ppermute | solution.py:30
  119.7 1.7 slice.481
  122.4 21.4 %collective-permute-done.11 = f32[3,3,1,128,128]{3,4,2,1,0:T(8,128)S(1)} collective-permute-done((f32[3,3,1,128,128]{3,4,2,1,0:T(8,128)}, f32[3,3,1,128,128]{3,4,2,1,0:T(8,128)S(1)}, u32[]{:S(2)}, u32[]{:S(2)}) %collective-permute-start.11) | collective-permute-done | bytes 589856 | tf_op jit(solution)/shard_map/ppermute | solution.py:32
  144.8 41.3 %gather_fusion.2 = f32[12288,128]{1,0:T(8,128)} fusion(f32[128,3968]{0,1:T(8,128)S(1)} %pad_maximum_fusion, s32[12288]{0:T(1024)S(1)} %broadcast_clamp_fusion), kind=kCustom, calls=%fused_computation.2 | custom fusion | bytes 12632064 | tf_op jit(solution)/shard_map/gather | solution.py:214
  186.1 6.8 %copy.144 = f32[24,512,128]{1,0,2:T(8,128)} copy(f32[24,512,128]{2,1,0:T(8,128)} %bitcast.281) | data formatting | bytes 12582912 | tf_op jit(solution)/shard_map/gather | solution.py:214
  192.8 4.1 %multiply_reduce_fusion.3 = (f32[16,24,512]{2,1,0:T(8,128)S(1)}, f32[16,24,512]{2,1,0:T(8,128)S(1)}, f32[8,24,512]{2,1,0:T(8,128)S(1)}) fusion(f32[8,24,512]{2,1,0:T(8,128)S(1)} %broadcast_multiply_fusion.2, f32[8,16,512]{2,1,0:T(8,128)S(1)} %copy.140, f32[8,16,24,512]{3,2,1,0:T(8,128)} %bitcast.277, f32[16,24,512]{2,1,0:T(8,128)S(1)} %copy-done.2), kind=kLoop, calls=%fused_computation.10 | loop fusion | flops 8945664 | bytes 9699328 | tf_op jit(solution)/shard_map/jvp()/reduce_sum | solution.py:109
  198.0 0.9 multiply_reduce_fusion
  199.3 1.0 convolution_bitcast_fusion
  201.2 3.8 %psum.35 = f32[11]{0:T(128)S(1)} all-reduce(f32[11]{0:T(128)S(1)} %pad_maximum_fusion.14), channel_id=1, replica_groups=mesh['gx_0'=2,'gx_1'=4,'gy_0'=8,'gy_1'=2,'gz'=4] {'gx_0'}, use_global_device_ids=true, to_apply=%region_14.15 | all-reduce | flops 11 | bytes 88 | tf_op jit(solution)/shard_map/psum | solution.py:40
  205.0 4.1 %scatter_custom_fusion.1 = f32[128]{0:T(128)S(1)} fusion(s32[512]{0:T(512)S(1)} %copy-done.9, f32[512]{0:T(512)S(1)} %fusion.251, f32[]{:T(128)} %constant.156.clone.1), kind=kCustom, calls=%fused_computation.570 | custom fusion | flops 512 | bytes 516 | tf_op jit(solution)/shard_map/scatter-add | solution.py:226
  209.0 6.0 %psum.36 = f32[11]{0:T(128)S(1)} all-reduce(f32[11]{0:T(128)S(1)} %psum.35), channel_id=1, replica_groups=mesh['gx_0'=2,'gx_1'=4,'gy_0'=8,'gy_1'=2,'gz'=4] {'gx_1'}, use_global_device_ids=true, to_apply=%region_15.16 | all-reduce | flops 11 | bytes 88 | tf_op jit(solution)/shard_map/psum | solution.py:40
  215.1 4.1 %scatter_custom_fusion = f32[128]{0:T(128)S(1)} fusion(s32[512]{0:T(512)S(1)} %copy-done.9, f32[512]{0:T(512)S(1)} %fusion.252, f32[]{:T(128)} %constant.156.clone.1), kind=kCustom, calls=%fused_computation.572 | custom fusion | flops 512 | bytes 516 | tf_op jit(solution)/shard_map/scatter-add | solution.py:223
  219.5 3.4 %collective-permute-start.12 = (f32[5,4,4,4]{3,2,1,0:T(4,128)S(1)}, f32[5,4,4,4]{3,2,1,0:T(4,128)S(1)}, u32[]{:S(2)}, u32[]{:S(2)}) collective-permute-start(f32[5,4,4,4]{3,2,1,0:T(4,128)S(1)} %get-tuple-element.51), channel_id=1, source_target_pairs={{0,64},{64,128},{128,192},{192,256},{256,320},{320,384},{384,448},... | collective-permute-start | bytes 3848 | tf_op jit(solution)/shard_map/ppermute | solution.py:30
  222.9 4.0 %collective-permute-start.13 = (f32[5,4,4,4]{3,2,1,0:T(4,128)S(1)}, f32[5,4,4,4]{3,2,1,0:T(4,128)S(1)}, u32[]{:S(2)}, u32[]{:S(2)}) collective-permute-start(f32[5,4,4,4]{3,2,1,0:T(4,128)S(1)} %get-tuple-element.52), channel_id=1, source_target_pairs={{64,0},{128,64},{192,128},{256,192},{320,256},{384,320},{448,384},... | collective-permute-start | bytes 3848 | tf_op jit(solution)/shard_map/ppermute | solution.py:32
  226.9 15.3 %psum.37 = f32[11]{0:T(128)S(1)} all-reduce(f32[11]{0:T(128)S(1)} %psum.36), channel_id=1, replica_groups=mesh['gx_0'=2,'gx_1'=4,'gy_0'=8,'gy_1'=2,'gz'=4] {'gy_0'}, use_global_device_ids=true, to_apply=%region_16.17 | all-reduce | flops 11 | bytes 88 | tf_op jit(solution)/shard_map/psum | solution.py:40
  242.2 9.5 %psum.38 = f32[11]{0:T(128)S(1)} all-reduce(f32[11]{0:T(128)S(1)} %psum.37), channel_id=1, replica_groups=mesh['gx_0'=2,'gx_1'=4,'gy_0'=8,'gy_1'=2,'gz'=4] {'gy_1'}, use_global_device_ids=true, to_apply=%region_17.18 | all-reduce | flops 11 | bytes 88 | tf_op jit(solution)/shard_map/psum | solution.py:40
  252.2 1.4 collective-permute-start.14
  253.6 9.6 %psum.39 = f32[11]{0:T(128)S(1)} all-reduce(f32[11]{0:T(128)S(1)} %psum.38), channel_id=1, replica_groups=mesh['gx_0'=2,'gx_1'=4,'gy_0'=8,'gy_1'=2,'gz'=4] {'gz'}, use_global_device_ids=true, to_apply=%region_18.19 | all-reduce | flops 11 | bytes 88 | tf_op jit(solution)/shard_map/psum | solution.py:40
  264.0 2.8 collective-permute-start.17
  266.7 3.4 %collective-permute-start.16 = (f32[5,4,12,16]{3,2,1,0:T(8,128)S(1)}, f32[5,4,12,16]{3,2,1,0:T(8,128)S(1)}, u32[]{:S(2)}, u32[]{:S(2)}) collective-permute-start(f32[5,4,12,16]{3,2,1,0:T(8,128)S(1)} %pad_maximum_fusion.5), channel_id=1, source_target_pairs={{0,1},{1,2},{2,3},{3,0},{4,5},{5,6},{6,7},{7,4},{8,9},{9,10},{10,1... | collective-permute-start | bytes 46088 | tf_op jit(solution)/shard_map/ppermute | solution.py:30
  270.2 1.2 slice_divide_fusion
  271.4 4.4 %collective-permute-done.17 = f32[5,4,12,16]{3,2,1,0:T(8,128)S(1)} collective-permute-done((f32[5,4,12,16]{3,2,1,0:T(8,128)S(1)}, f32[5,4,12,16]{3,2,1,0:T(8,128)S(1)}, u32[]{:S(2)}, u32[]{:S(2)}) %collective-permute-start.17) | collective-permute-done | bytes 15392 | tf_op jit(solution)/shard_map/ppermute | solution.py:32
  275.8 4.3 %collective-permute-done.16 = f32[5,4,12,16]{3,2,1,0:T(8,128)S(1)} collective-permute-done((f32[5,4,12,16]{3,2,1,0:T(8,128)S(1)}, f32[5,4,12,16]{3,2,1,0:T(8,128)S(1)}, u32[]{:S(2)}, u32[]{:S(2)}) %collective-permute-start.16) | collective-permute-done | bytes 15392 | tf_op jit(solution)/shard_map/ppermute | solution.py:30
  282.0 3.3 %gather_fusion.3 = f32[512]{0:T(512)S(1)} fusion(f32[128]{0:T(128)S(1)} %reshape.674, s32[1024]{0:T(1024)S(1)} %get-tuple-element.59), kind=kCustom, calls=%fused_computation.3 | custom fusion | bytes 6144 | tf_op jit(solution)/shard_map/jit(_take)/gather | solution.py:258
  (168 shorter events, 23.9 us)
Async XLA Ops:
  0.6 45.9 %copy-start = (f32[16,8]{0,1:T(8,128)S(1)}, f32[16,8]{0,1:T(8,128)}, u32[]{:S(2)}) copy-start(f32[16,8]{0,1:T(8,128)} %param.20) | copy-start | bytes 1540
  0.6 43.8 %copy-start.6 = (f32[3,512]{1,0:T(4,128)S(1)}, f32[3,512]{1,0:T(4,128)}, u32[]{:S(2)}) copy-start(f32[3,512]{1,0:T(4,128)} %param.13) | copy-start | bytes 18436
  4.3 15.1 %collective-permute-start.1 = (f32[1,1,1,3,128]{3,4,2,1,0:T(8,128)S(1)}, f32[1,1,1,3,128]{3,4,2,1,0:T(8,128)S(1)}, u32[]{:S(2)}, u32[]{:S(2)}) collective-permute-start(f32[1,1,1,3,128]{3,4,2,1,0:T(8,128)S(1)} %bitcast_select_fusion.1), channel_id=1, source_target_pairs={{64,0},{128,64},{192,128},{256,192},{320,256},{384,320},{448,384},... | collective-permute-start | bytes 4616 | tf_op jit(solution)/shard_map/ppermute | solution.py:32
  11.3 8.2 %collective-permute-start = (f32[1,1,1,3,128]{3,4,2,1,0:T(8,128)S(1)}, f32[1,1,1,3,128]{3,4,2,1,0:T(8,128)S(1)}, u32[]{:S(2)}, u32[]{:S(2)}) collective-permute-start(f32[1,1,1,3,128]{3,4,2,1,0:T(8,128)S(1)} %bitcast_select_fusion.1), channel_id=1, source_target_pairs={{0,64},{64,128},{128,192},{192,256},{256,320},{320,384},{384,448},... | collective-permute-start | bytes 4616 | tf_op jit(solution)/shard_map/ppermute | solution.py:30
  19.6 4.6 %collective-permute-start.3 = (f32[3,1,1,3,128]{4,2,3,1,0:T(1,128)S(1)}, f32[3,1,1,3,128]{4,2,3,1,0:T(1,128)S(1)}, u32[]{:S(2)}, u32[]{:S(2)}) collective-permute-start(f32[3,1,1,3,128]{4,2,3,1,0:T(1,128)S(1)} %pad_maximum_fusion.13), channel_id=1, source_target_pairs={{4,0},{8,4},{12,8},{16,12},{20,16},{24,20},{28,24},{32,28},{36,32}... | collective-permute-start | bytes 13832 | tf_op jit(solution)/shard_map/ppermute | solution.py:32
  23.4 1.2 collective-permute-start.2
  24.5 11.2 %collective-permute-start.5 = (f32[3,3,1,3,128]{4,2,3,1,0:T(1,128)S(1)}, f32[3,3,1,3,128]{4,2,3,1,0:T(1,128)S(1)}, u32[]{:S(2)}, u32[]{:S(2)}) collective-permute-start(f32[3,3,1,3,128]{4,2,3,1,0:T(1,128)S(1)} %pad_maximum_fusion.12), channel_id=1, source_target_pairs={{1,0},{2,1},{3,2},{0,3},{5,4},{6,5},{7,6},{4,7},{9,8},{10,9},{11,1... | collective-permute-start | bytes 41480 | tf_op jit(solution)/shard_map/ppermute | solution.py:32
  33.6 6.6 %collective-permute-start.4 = (f32[3,3,1,3,128]{4,2,3,1,0:T(1,128)S(1)}, f32[3,3,1,3,128]{4,2,3,1,0:T(1,128)S(1)}, u32[]{:S(2)}, u32[]{:S(2)}) collective-permute-start(f32[3,3,1,3,128]{4,2,3,1,0:T(1,128)S(1)} %pad_maximum_fusion.12), channel_id=1, source_target_pairs={{0,1},{1,2},{2,3},{3,0},{4,5},{5,6},{6,7},{7,4},{8,9},{9,10},{10,1... | collective-permute-start | bytes 41480 | tf_op jit(solution)/shard_map/ppermute | solution.py:30
  45.5 9.5 %copy-start.1 = (f32[16,24,512]{2,1,0:T(8,128)}, f32[16,24,512]{2,1,0:T(8,128)S(1)}, u32[]{:S(2)}) copy-start(f32[16,24,512]{2,1,0:T(8,128)S(1)} %constant_dynamic-update-slice_fusion) | copy-start | bytes 2359300
  45.8 0.7 copy-start.3
  84.7 25.3 %copy-start.10 = (f32[4,4,8]{2,1,0:T(4,128)S(1)}, f32[4,4,8]{2,1,0:T(4,128)}, u32[]{:S(2)}) copy-start(f32[4,4,8]{2,1,0:T(4,128)} %param.24) | copy-start | bytes 1540
  84.7 35.0 %copy-start.11 = (f32[4,4,8]{2,1,0:T(4,128)S(1)}, f32[4,4,8]{2,1,0:T(4,128)}, u32[]{:S(2)}) copy-start(f32[4,4,8]{2,1,0:T(4,128)} %param.25) | copy-start | bytes 1540
  84.8 36.7 %copy-start.12 = (f32[16]{0:T(128)S(1)}, f32[16]{0:T(128)}, u32[]{:S(2)}) copy-start(f32[16]{0:T(128)} %param.21) | copy-start | bytes 196
  90.8 7.6 %collective-permute-start.7 = (f32[1,1,1,128,128]{3,4,2,1,0:T(8,128)S(1)}, f32[1,1,1,128,128]{3,4,2,1,0:T(8,128)S(1)}, u32[]{:S(2)}, u32[]{:S(2)}) collective-permute-start(f32[1,1,1,128,128]{3,4,2,1,0:T(8,128)S(1)} %bitcast_select_fusion), channel_id=1, source_target_pairs={{64,0},{128,64},{192,128},{256,192},{320,256},{384,320},{448,384},... | collective-permute-start | bytes 196616 | tf_op jit(solution)/shard_map/ppermute | solution.py:32
  96.4 7.1 %collective-permute-start.6 = (f32[1,1,1,128,128]{3,4,2,1,0:T(8,128)S(1)}, f32[1,1,1,128,128]{3,4,2,1,0:T(8,128)S(1)}, u32[]{:S(2)}, u32[]{:S(2)}) collective-permute-start(f32[1,1,1,128,128]{3,4,2,1,0:T(8,128)S(1)} %bitcast_select_fusion), channel_id=1, source_target_pairs={{0,64},{64,128},{128,192},{192,256},{256,320},{320,384},{384,448},... | collective-permute-start | bytes 196616 | tf_op jit(solution)/shard_map/ppermute | solution.py:30
  103.6 7.5 %collective-permute-start.9 = (f32[3,1,1,128,128]{3,4,2,1,0:T(8,128)S(1)}, f32[3,1,1,128,128]{3,4,2,1,0:T(8,128)S(1)}, u32[]{:S(2)}, u32[]{:S(2)}) collective-permute-start(f32[3,1,1,128,128]{3,4,2,1,0:T(8,128)S(1)} %pad_maximum_fusion.4), channel_id=1, source_target_pairs={{4,0},{8,4},{12,8},{16,12},{20,16},{24,20},{28,24},{32,28},{36,32}... | collective-permute-start | bytes 589832 | tf_op jit(solution)/shard_map/ppermute | solution.py:32
  110.0 2.6 collective-permute-start.8
  113.5 30.3 %collective-permute-start.11 = (f32[3,3,1,128,128]{3,4,2,1,0:T(8,128)}, f32[3,3,1,128,128]{3,4,2,1,0:T(8,128)S(1)}, u32[]{:S(2)}, u32[]{:S(2)}) collective-permute-start(f32[3,3,1,128,128]{3,4,2,1,0:T(8,128)} %pad_maximum_fusion.2), channel_id=1, source_target_pairs={{1,0},{2,1},{3,2},{0,3},{5,4},{6,5},{7,6},{4,7},{9,8},{10,9},{11,1... | collective-permute-start | bytes 1769480 | tf_op jit(solution)/shard_map/ppermute | solution.py:32
  115.4 29.1 %collective-permute-start.10 = (f32[3,3,1,128,128]{3,4,2,1,0:T(8,128)}, f32[3,3,1,128,128]{3,4,2,1,0:T(8,128)S(1)}, u32[]{:S(2)}, u32[]{:S(2)}) collective-permute-start(f32[3,3,1,128,128]{3,4,2,1,0:T(8,128)} %pad_maximum_fusion.2), channel_id=1, source_target_pairs={{0,1},{1,2},{2,3},{3,0},{4,5},{5,6},{6,7},{7,4},{8,9},{9,10},{10,1... | collective-permute-start | bytes 1769480 | tf_op jit(solution)/shard_map/ppermute | solution.py:30
  186.1 6.8 %copy-start.2 = (f32[16,24,512]{2,1,0:T(8,128)S(1)}, f32[16,24,512]{2,1,0:T(8,128)}, u32[]{:S(2)}) copy-start(f32[16,24,512]{2,1,0:T(8,128)} %copy-done.1) | copy-start | bytes 2359300
  192.8 5.1 %slice-start = ((s8[6291456]{0:T(1024)(128)(4,1)}), s8[4194304]{0:T(1024)(128)(4,1)S(1)}, s32[]{:S(2)}) async-start(s8[6291456]{0:T(1024)(128)(4,1)} %bitcast.278), calls=%async_computation | async-start | bytes 8388608
  192.8 4.5 %copy-start.5 = (f32[16,24,512]{2,1,0:T(8,128)S(1)}, f32[16,24,512]{2,1,0:T(8,128)}, u32[]{:S(2)}) copy-start(f32[16,24,512]{2,1,0:T(8,128)} %get-tuple-element.27) | copy-start | bytes 2359300
  192.8 5.1 %slice-start.1 = ((s8[6291456]{0:T(1024)(128)(4,1)}), s8[2097152]{0:T(1024)(128)(4,1)S(1)}, s32[]{:S(2)}) async-start(s8[6291456]{0:T(1024)(128)(4,1)} %bitcast.278), calls=%async_computation.1 | async-start | bytes 4194304
  197.8 1.0 copy-start.4
  197.9 7.0 %copy-start.9 = (s32[512]{0:T(512)S(1)}, s32[512]{0:T(512)}, u32[]{:S(2)}) copy-start(s32[512]{0:T(512)} %param.19) | copy-start | bytes 6148
  198.0 17.1 %copy-start.8 = (f32[3,512]{1,0:T(4,128)S(1)}, f32[3,512]{1,0:T(4,128)}, u32[]{:S(2)}) copy-start(f32[3,512]{1,0:T(4,128)} %param.14) | copy-start | bytes 18436
  199.3 86.1 %copy-start.7 = (f32[3,512]{1,0:T(4,128)}, f32[3,512]{1,0:T(4,128)S(1)}, u32[]{:S(2)}) copy-start(f32[3,512]{1,0:T(4,128)S(1)} %get-tuple-element.25) | copy-start | bytes 18436
  219.5 32.3 %collective-permute-start.12 = (f32[5,4,4,4]{3,2,1,0:T(4,128)S(1)}, f32[5,4,4,4]{3,2,1,0:T(4,128)S(1)}, u32[]{:S(2)}, u32[]{:S(2)}) collective-permute-start(f32[5,4,4,4]{3,2,1,0:T(4,128)S(1)} %get-tuple-element.51), channel_id=1, source_target_pairs={{0,64},{64,128},{128,192},{192,256},{256,320},{320,384},{384,448},... | collective-permute-start | bytes 3848 | tf_op jit(solution)/shard_map/ppermute | solution.py:30
  222.9 28.9 %collective-permute-start.13 = (f32[5,4,4,4]{3,2,1,0:T(4,128)S(1)}, f32[5,4,4,4]{3,2,1,0:T(4,128)S(1)}, u32[]{:S(2)}, u32[]{:S(2)}) collective-permute-start(f32[5,4,4,4]{3,2,1,0:T(4,128)S(1)} %get-tuple-element.52), channel_id=1, source_target_pairs={{64,0},{128,64},{192,128},{256,192},{320,256},{384,320},{448,384},... | collective-permute-start | bytes 3848 | tf_op jit(solution)/shard_map/ppermute | solution.py:32
  251.9 11.9 %collective-permute-start.15 = (f32[5,4,4,16]{3,2,1,0:T(4,128)S(1)}, f32[5,4,4,16]{3,2,1,0:T(4,128)S(1)}, u32[]{:S(2)}, u32[]{:S(2)}) collective-permute-start(f32[5,4,4,16]{3,2,1,0:T(4,128)S(1)} %pad_maximum_fusion.11), channel_id=1, source_target_pairs={{4,0},{8,4},{12,8},{16,12},{20,16},{24,20},{28,24},{32,28},{36,32}... | collective-permute-start | bytes 15368 | tf_op jit(solution)/shard_map/ppermute | solution.py:32
  252.2 11.6 %collective-permute-start.14 = (f32[5,4,4,16]{3,2,1,0:T(4,128)S(1)}, f32[5,4,4,16]{3,2,1,0:T(4,128)S(1)}, u32[]{:S(2)}, u32[]{:S(2)}) collective-permute-start(f32[5,4,4,16]{3,2,1,0:T(4,128)S(1)} %pad_maximum_fusion.11), channel_id=1, source_target_pairs={{0,4},{4,8},{8,12},{12,16},{16,20},{20,24},{24,28},{28,32},{32,36}... | collective-permute-start | bytes 15368 | tf_op jit(solution)/shard_map/ppermute | solution.py:30
  264.0 11.8 %collective-permute-start.17 = (f32[5,4,12,16]{3,2,1,0:T(8,128)S(1)}, f32[5,4,12,16]{3,2,1,0:T(8,128)S(1)}, u32[]{:S(2)}, u32[]{:S(2)}) collective-permute-start(f32[5,4,12,16]{3,2,1,0:T(8,128)S(1)} %pad_maximum_fusion.5), channel_id=1, source_target_pairs={{1,0},{2,1},{3,2},{0,3},{5,4},{6,5},{7,6},{4,7},{9,8},{10,9},{11,1... | collective-permute-start | bytes 46088 | tf_op jit(solution)/shard_map/ppermute | solution.py:32
  266.7 13.4 %collective-permute-start.16 = (f32[5,4,12,16]{3,2,1,0:T(8,128)S(1)}, f32[5,4,12,16]{3,2,1,0:T(8,128)S(1)}, u32[]{:S(2)}, u32[]{:S(2)}) collective-permute-start(f32[5,4,12,16]{3,2,1,0:T(8,128)S(1)} %pad_maximum_fusion.5), channel_id=1, source_target_pairs={{0,1},{1,2},{2,3},{3,0},{4,5},{5,6},{6,7},{7,4},{8,9},{9,10},{10,1... | collective-permute-start | bytes 46088 | tf_op jit(solution)/shard_map/ppermute | solution.py:30
